TPU v7x, 768 devices: a whole 4x8x12 slice. The times are simulated.
768 devices in a mesh: shard: 48 (over z, x), cache: 16 (over y, core).
Axes of the slice: x: 4, y: 8, z: 12, core: 2. Of those that a mesh axis runs over, the one named last changes fastest.
Arguments:
- table: bfloat16 [786432, 256], P(('shard', 'cache'))
- panel_ids: int32 [2304], P(('shard', 'cache')), may hold values from 0 to 7, as said below
- bag_slots: int32 [16, 196608, 16], P('cache', 'shard'), may hold values from 0 to 2047
- block_ids: int32 [16, 1536, 16], P('cache', 'shard'), may hold values from 0 to 55
- bag_counts: int32 [16, 1536], P('cache', 'shard'), may hold values from 1 to 16, as said below
- dense_owner: int32 [768], P('shard'), may hold values from 0 to 15, as said below
- top_weight: bfloat16 [256, 1024], replicated, may hold values from -0.375 to 0.375
- bn_gain: float32 [1024], replicated, may hold values from 0.1 to 1.9
- bn_shift: float32 [1024], replicated, may hold values from -3 to 3
- out_weight: bfloat16 [1024], replicated, may hold values from -0.1875 to 0.1875
Outputs:
- top_hidden: bfloat16 [196608, 1024], P(('shard', 'cache'))
- logits: float32 [196608], P(('shard', 'cache'))
Inputs may be any that keep to these rules, and one draw needn't show every extreme that they name: `bag_slots`: an entry v names row v % 128 of the block in place v // 128 of its bag block's list; places at or beyond the list's count are unused. `block_ids`: values below 48 name hot blocks of the group, the others own blocks of the feature's device. `bag_counts`: some bag block uses all 16 places. `panel_ids`: distinct within a device. `dense_owner`: each group of 16 consecutive entries is a permutation.
All inputs are finite; a program needn't handle non-finite values.
Results may differ from a plain program's by a relative error of at most 0.0055.
Values may be sent and summed in bfloat16 or wider, within the bound.
No kernel may reach another device: no remote copies, remote signals or barrier semaphores. Data moves between devices by JAX's collectives and lax.ppermute only.
A program may use at most 128 MiB of HBM per device.

v0:
```python
import math

import jax
import jax.numpy as jnp
from jax import lax
from jax.sharding import PartitionSpec as P

norm_eps = 1e-05


def shards(
    table,
    panel_ids,
    bag_slots,
    block_ids,
    bag_counts,
    dense_owner,
    top_weight,
    bn_gain,
    bn_shift,
    out_weight,
):
    row_width = table.shape[1]
    caches = lax.axis_size("cache")
    feat_dev, group_samp, bag_len = bag_slots.shape
    samp_dev = group_samp // caches
    owner_blocks = samp_dev // 128
    group_blocks = group_samp // 128
    blocks_dev = feat_dev * group_blocks
    list_len = block_ids.shape[2]
    table_blocks = table.shape[0] // 128
    hot_rows = jnp.take(table.reshape(-1, 128, row_width), panel_ids, axis=0).reshape(-1, row_width)
    hot_blocks = hot_rows.shape[0] // 128 * caches
    cache_ids = jnp.arange(caches, dtype=jnp.int32)
    owner_match = dense_owner[None, :] == cache_ids[:, None]
    inverse = jnp.sum(jnp.where(owner_match, cache_ids[None, :], 0), axis=1)
    block_number = jnp.arange(blocks_dev, dtype=jnp.int32)
    feature_part = block_number // group_blocks
    within_group = block_number % group_blocks
    source_block = (
        feature_part * group_blocks
        + inverse[within_group // owner_blocks] * owner_blocks
        + within_group % owner_blocks
    )
    batch_blocks = math.gcd(4, blocks_dev)
    batch_count = blocks_dev // batch_blocks
    slot_blocks = jnp.take(bag_slots.reshape(blocks_dev, 128, bag_len), source_block, axis=0)
    list_ids = jnp.take(block_ids.reshape(blocks_dev, list_len), source_block, axis=0)
    list_counts = jnp.take(bag_counts.reshape(blocks_dev), source_block, axis=0)
    grouped = (
        slot_blocks.reshape(batch_count, batch_blocks, 128, bag_len),
        list_ids.reshape(batch_count, batch_blocks, list_len),
        list_counts.reshape(batch_count, batch_blocks),
    )
    lane_ids = jnp.arange(list_len * 128, dtype=jnp.int32)
    place_ids = jnp.arange(list_len, dtype=jnp.int32)
    gathered = lax.all_gather(hot_rows, "cache", axis=0, tiled=True)
    source = jnp.concatenate([gathered, table], axis=0).reshape(
        hot_blocks + table_blocks, 128, row_width
    )
    block_total = hot_blocks + table_blocks

    def one_batch(members):
        slots, names, counts = members
        incidence = jnp.sum((slots[..., None] == lane_ids).astype(jnp.float32), axis=2)
        live = (place_ids[None, :] < counts[:, None]) & (names >= 0) & (names < 0 + block_total)
        incidence = incidence.reshape(batch_blocks, 128, list_len, 128) * live[
            :, None, :, None
        ].astype(jnp.float32)
        matches = incidence.astype(jnp.bfloat16)
        picks = jnp.clip(names - 0, 0, block_total - 1)
        panel_rows = jnp.take(source, picks, axis=0)
        return jnp.einsum("bskr,bkre->bse", matches, panel_rows, preferred_element_type=jnp.float32)

    pooled_sum = lax.map(one_batch, grouped).reshape(blocks_dev, 128, row_width)
    pooled = pooled_sum.reshape(feat_dev, caches, samp_dev, row_width).astype(jnp.bfloat16)
    features = lax.all_to_all(pooled, "cache", split_axis=1, concat_axis=0, tiled=True)[:, 0]
    products = jnp.einsum("fne,gne->nfg", features, features, preferred_element_type=jnp.float32)
    interaction = (products / math.sqrt(row_width)).astype(jnp.bfloat16)
    flat_rows = interaction.reshape(interaction.shape[0], -1)
    pre_norm = jnp.dot(flat_rows, top_weight, preferred_element_type=jnp.float32)
    sample_count = pre_norm.shape[0] * lax.axis_size("shard") * caches
    col_mean = lax.psum(jnp.sum(pre_norm, axis=0), ("shard", "cache")) / sample_count
    centered = pre_norm - col_mean
    col_var = lax.psum(jnp.sum(centered * centered, axis=0), ("shard", "cache")) / sample_count
    normed = (pre_norm - col_mean) * lax.rsqrt(col_var + norm_eps) * bn_gain + bn_shift
    top_hidden = jax.nn.relu(normed).astype(jnp.bfloat16)
    logits = jnp.dot(top_hidden, out_weight, preferred_element_type=jnp.float32)
    return (top_hidden, logits)


def solution(mesh):
    return jax.shard_map(
        shards,
        mesh=mesh,
        in_specs=(
            P(("shard", "cache"), None),
            P(("shard", "cache")),
            P("cache", "shard", None),
            P("cache", "shard", None),
            P("cache", "shard"),
            P("shard"),
            P(),
            P(),
            P(),
            P(),
        ),
        out_specs=(P(("shard", "cache"), None), P(("shard", "cache"))),
        check_vma=False,
    )
```

profile of v0, /device:TPU:6, one launch (start us, length us, event | category | flops | bytes accessed | tf_op | source)
XLA Modules:
  0.0 626.1 jit_solution(5937744424057953216)
XLA Ops:
  17.6 46.1 %all-gather.2.cloned.1.call-done = bf16[6144,256]{1,0:T(8,128)(2,1)} async-done(((bf16[384,256]{1,0:T(8,128)(2,1)}), bf16[6144,256]{1,0:T(8,128)(2,1)}) %all-gather.2.cloned.1.call-update) | async-done | bytes 3145744 | tf_op jit(solution)/shard_map/all_gather | solution.py:57
  67.7 277.7 %while.11 = (s32[]{:T(128)}, bf16[8,4,128,256]{3,2,1,0:T(8,128)(2,1)}, s32[8,4,128,16]{2,3,1,0:T(8,128)S(1)}, s32[8,4]{1,0:T(8,128)S(1)}, s32[8,4,16]{2,1,0:T(4,...) while((s32[]{:T(128)}, bf16[8,4,128,256]{3,2,1,0:T(8,128)(2,1)}, ...), condition=%wide.region_3.4_spmd.clone, body=%wide.region_1.3_spmd.clone.sunk | while | flops 590350400 | bytes 30054936 | solution.py:75
  68.0 18.6 %convert_reduce_fusion.2 = f32[4,128,2048]{2,1,0:T(8,128)} fusion(s32[4,128,16]{2,1,0:T(8,128)S(1)} %copy.56), kind=kLoop, calls=%fused_computation.9.clone.1 | loop fusion | flops 49283072 | bytes 4227072 | tf_op jit(solution)/shard_map/while/body/eval_jaxpr/reduce_sum | solution.py:65
  86.6 5.3 copy.57
  96.7 5.7 fusion.55
  102.7 18.6 %convert_reduce_fusion.2 = f32[4,128,2048]{2,1,0:T(8,128)} fusion(s32[4,128,16]{2,1,0:T(8,128)S(1)} %copy.56), kind=kLoop, calls=%fused_computation.9.clone.1 | loop fusion | flops 49283072 | bytes 4227072 | tf_op jit(solution)/shard_map/while/body/eval_jaxpr/reduce_sum | solution.py:65
  121.3 5.3 copy.57
  126.6 4.8 gather_fusion
  131.4 5.7 fusion.55
  137.4 18.6 %convert_reduce_fusion.2 = f32[4,128,2048]{2,1,0:T(8,128)} fusion(s32[4,128,16]{2,1,0:T(8,128)S(1)} %copy.56), kind=kLoop, calls=%fused_computation.9.clone.1 | loop fusion | flops 49283072 | bytes 4227072 | tf_op jit(solution)/shard_map/while/body/eval_jaxpr/reduce_sum | solution.py:65
  156.0 5.3 copy.57
  166.2 5.7 fusion.55
  172.1 18.6 %convert_reduce_fusion.2 = f32[4,128,2048]{2,1,0:T(8,128)} fusion(s32[4,128,16]{2,1,0:T(8,128)S(1)} %copy.56), kind=kLoop, calls=%fused_computation.9.clone.1 | loop fusion | flops 49283072 | bytes 4227072 | tf_op jit(solution)/shard_map/while/body/eval_jaxpr/reduce_sum | solution.py:65
  190.7 5.3 copy.57
  196.1 4.8 gather_fusion
  200.9 5.7 fusion.55
  206.9 18.6 %convert_reduce_fusion.2 = f32[4,128,2048]{2,1,0:T(8,128)} fusion(s32[4,128,16]{2,1,0:T(8,128)S(1)} %copy.56), kind=kLoop, calls=%fused_computation.9.clone.1 | loop fusion | flops 49283072 | bytes 4227072 | tf_op jit(solution)/shard_map/while/body/eval_jaxpr/reduce_sum | solution.py:65
  225.4 5.3 copy.57
  235.6 5.7 fusion.55
  241.6 18.6 %convert_reduce_fusion.2 = f32[4,128,2048]{2,1,0:T(8,128)} fusion(s32[4,128,16]{2,1,0:T(8,128)S(1)} %copy.56), kind=kLoop, calls=%fused_computation.9.clone.1 | loop fusion | flops 49283072 | bytes 4227072 | tf_op jit(solution)/shard_map/while/body/eval_jaxpr/reduce_sum | solution.py:65
  260.2 5.3 copy.57
  265.5 4.8 gather_fusion
  270.3 5.7 fusion.55
  276.3 18.6 %convert_reduce_fusion.2 = f32[4,128,2048]{2,1,0:T(8,128)} fusion(s32[4,128,16]{2,1,0:T(8,128)S(1)} %copy.56), kind=kLoop, calls=%fused_computation.9.clone.1 | loop fusion | flops 49283072 | bytes 4227072 | tf_op jit(solution)/shard_map/while/body/eval_jaxpr/reduce_sum | solution.py:65
  294.9 5.3 copy.57
  305.1 5.7 fusion.55
  311.0 18.6 %convert_reduce_fusion.2 = f32[4,128,2048]{2,1,0:T(8,128)} fusion(s32[4,128,16]{2,1,0:T(8,128)S(1)} %copy.56), kind=kLoop, calls=%fused_computation.9.clone.1 | loop fusion | flops 49283072 | bytes 4227072 | tf_op jit(solution)/shard_map/while/body/eval_jaxpr/reduce_sum | solution.py:65
  329.6 5.3 copy.57
  339.8 5.6 fusion.55
  350.0 49.2 %all-to-all-done = bf16[1,16,256,256]{3,2,0,1:T(8,128)(2,1)S(1)} async-done(((bf16[1,16,256,256]{3,2,0,1:T(8,128)(2,1)}), bf16[1,16,256,256]{3,2,0,1:T(8,128)(2,1)S(1)}, u32[]{:S(2)}, u32[]{:S(2)}) %all-to-all-start) | async-done | bytes 2097184 | tf_op jit(solution)/shard_map/all_to_all | solution.py:77
  404.8 108.5 %psum.14 = f32[1024]{0:T(1024)S(1)} all-reduce(f32[1024]{0:T(1024)S(1)} %get-tuple-element.74), channel_id=1, replica_groups=mesh['shard'=48,'cache'=16] {'shard','cache'}, use_global_device_ids=true, to_apply=%region_5.6 | all-reduce | flops 1024 | bytes 8192 | tf_op jit(solution)/shard_map/psum | solution.py:83
  513.4 104.9 %psum.15 = f32[1024]{0:T(1024)S(1)} all-reduce(f32[1024]{0:T(1024)S(1)} %multiply_reduce_fusion), channel_id=1, replica_groups=mesh['shard'=48,'cache'=16] {'shard','cache'}, use_global_device_ids=true, to_apply=%region_7.8 | all-reduce | flops 1024 | bytes 8192 | tf_op jit(solution)/shard_map/psum | solution.py:85
  (113 shorter events, 52.0 us)
Async XLA Ops:
  7.2 397.2 %copy-start = (bf16[256,1024]{1,0:T(8,128)(2,1)S(1)}, bf16[256,1024]{1,0:T(8,128)(2,1)}, u32[]{:S(2)}) copy-start(bf16[256,1024]{1,0:T(8,128)(2,1)} %param.18) | copy-start | bytes 1572868
  7.2 56.5 %all-gather.2.cloned.1.call-start = ((), (), s32[]{:S(2)}) async-start(), calls=%async_computation.1 | async-start | bytes 3342336 | tf_op jit(solution)/shard_map/all_gather | solution.py:57
  11.1 52.6 %copy-start.2 = (bf16[1024,256]{1,0:T(8,128)(2,1)S(1)}, bf16[1024,256]{1,0:T(8,128)(2,1)}, u32[]{:S(2)}) copy-start(bf16[1024,256]{1,0:T(8,128)(2,1)} %param.12) | copy-start | bytes 1572868
  345.4 4.6 copy-start.5
  345.4 53.8 %all-to-all-start = ((bf16[1,16,256,256]{3,2,0,1:T(8,128)(2,1)}), bf16[1,16,256,256]{3,2,0,1:T(8,128)(2,1)S(1)}, u32[]{:S(2)}, u32[]{:S(2)}) async-start(bf16[1,16,256,256]{3,2,0,1:T(8,128)(2,1)} %bitcast.80), calls=%async_computation | async-start | bytes 4194304 | tf_op jit(solution)/shard_map/all_to_all | solution.py:77
  401.9 216.4 %copy-start.3 = (f32[1024]{0:T(1024)S(1)}, f32[1024]{0:T(1024)}, u32[]{:S(2)}) copy-start(f32[1024]{0:T(1024)} %param.20) | copy-start | bytes 12292
  401.9 216.4 %copy-start.4 = (f32[1024]{0:T(1024)S(1)}, f32[1024]{0:T(1024)}, u32[]{:S(2)}) copy-start(f32[1024]{0:T(1024)} %param.19) | copy-start | bytes 12292
  618.4 0.8 copy-start.1
Sparse Core Ops, SparseCore 0:
  11.2 52.4 all-gather.1
where the time goes:
time: 629 us; the launch traced here: 626 us
  blocking collectives  213 us (34%)
  other arithmetic  157 us (25%)
  waiting for transfers between devices  95.3 us (15%)
  local copies, waits for them, and re-layouts  92.6 us (15%)
  matrix products  49.1 us (8%)
  between operations  14.2 us (2%)
    reduce_sum x8, other arithmetic, one_batch(): jnp.sum((slots[..., None] == lane_ids).astype(jnp.float32), axis=2)  149 us
    psum x1, blocking collectives, shards(): lax.psum(jnp.sum(pre_norm, axis=0), ('shard', 'cache')) / sample_count  108 us
    psum x1, blocking collectives, shards(): lax.psum(jnp.sum(centered * centered, axis=0), ('shard', 'cache'))  105 us
    all_to_all x1, waiting for transfers between devices, shards(): lax.all_to_all(pooled, 'cache', split_axis=1, concat_axis=0, tiled=True)  49.2 us
    all_gather x1, waiting for transfers between devices, shards(): gathered = lax.all_gather(hot_rows, 'cache', axis=0, tiled=True)  46.1 us
    dot_general x8, matrix products, one_batch(): jnp.einsum('bskr,bkre->bse', matches, panel_rows, preferred_element_type=...  45.3 us
    reduce_sum x8, local copies, waits for them, and re-layouts, one_batch(): jnp.sum((slots[..., None] == lane_ids).astype(jnp.float32), axis=2)  42.8 us
    gather x8, local copies, waits for them, and re-layouts, one_batch(): panel_rows = jnp.take(source, picks, axis=0)  38.6 us
  transfers between devices with their start and end apart: 2, of which 2 were waited for; matrix products, arithmetic and copies ran while one was open for 1% of the time, Pallas kernels for 0%

commit v1 on v0

v1 whole, which is shorter than its diff:
```python
import functools
import math

import jax
import jax.numpy as jnp
from jax import lax
from jax.experimental import pallas as pl
from jax.experimental.pallas import tpu as pltpu
from jax.sharding import PartitionSpec as P

norm_eps = 1e-05


def pool_kernel(order_ref, ids_ref, counts_ref, slots_ref, hot_ref, own_ref, out_ref, acc_ref):
    step = pl.program_id(0)
    block = order_ref[step]
    list_len = slots_ref.shape[1]
    hot_count = hot_ref.shape[0] // 128
    own_count = own_ref.shape[0] // 128
    slots = slots_ref[0]
    row_iota = lax.broadcasted_iota(jnp.int32, (128, 128), 0)
    acc_ref[...] = jnp.zeros(acc_ref.shape, jnp.float32)

    def place(k, carry):
        shifted = slots - k * 128
        hits = jnp.zeros((128, 128), jnp.float32)
        for entry in range(list_len):
            hits = hits + (shifted[entry : entry + 1, :] == row_iota).astype(jnp.float32)
        name = jnp.clip(ids_ref[block * list_len + k], 0, hot_count + own_count - 1)
        hot_start = pl.multiple_of(jnp.minimum(name, hot_count - 1) * 128, 128)
        own_start = pl.multiple_of(jnp.maximum(name - hot_count, 0) * 128, 128)
        rows = jnp.where(
            name < hot_count,
            hot_ref[pl.ds(hot_start, 128), :],
            own_ref[pl.ds(own_start, 128), :],
        )
        acc_ref[...] += lax.dot_general(
            hits.astype(jnp.bfloat16),
            rows,
            (((0,), (0,)), ((), ())),
            preferred_element_type=jnp.float32,
        )
        return carry

    count = jnp.clip(counts_ref[block], 0, list_len)
    lax.fori_loop(0, count, place, 0)
    out_ref[...] = acc_ref[...].astype(out_ref.dtype)


def pool(order, ids, counts, slots_t, hot, own):
    blocks, bag_len, _ = slots_t.shape
    width = hot.shape[1]
    grid_spec = pltpu.PrefetchScalarGridSpec(
        num_scalar_prefetch=3,
        grid=(blocks,),
        in_specs=[
            pl.BlockSpec((1, bag_len, 128), lambda i, o, d, c: (o[i], 0, 0)),
            pl.BlockSpec(hot.shape, lambda i, o, d, c: (0, 0)),
            pl.BlockSpec(own.shape, lambda i, o, d, c: (0, 0)),
        ],
        out_specs=pl.BlockSpec((128, width), lambda i, o, d, c: (i, 0)),
        scratch_shapes=[pltpu.VMEM((128, width), jnp.float32)],
    )
    return pl.pallas_call(
        pool_kernel,
        grid_spec=grid_spec,
        out_shape=jax.ShapeDtypeStruct((blocks * 128, width), jnp.bfloat16),
        compiler_params=pltpu.CompilerParams(
            dimension_semantics=("arbitrary",), vmem_limit_bytes=40 * 1024 * 1024
        ),
    )(order, ids, counts, slots_t, hot, own)


def shards(
    table,
    panel_ids,
    bag_slots,
    block_ids,
    bag_counts,
    dense_owner,
    top_weight,
    bn_gain,
    bn_shift,
    out_weight,
):
    row_width = table.shape[1]
    caches = lax.axis_size("cache")
    feat_dev, group_samp, bag_len = bag_slots.shape
    samp_dev = group_samp // caches
    owner_blocks = samp_dev // 128
    group_blocks = group_samp // 128
    blocks_dev = feat_dev * group_blocks
    list_len = block_ids.shape[2]
    hot_rows = jnp.take(table.reshape(-1, 128, row_width), panel_ids, axis=0).reshape(-1, row_width)
    cache_ids = jnp.arange(caches, dtype=jnp.int32)
    owner_match = dense_owner[None, :] == cache_ids[:, None]
    inverse = jnp.sum(jnp.where(owner_match, cache_ids[None, :], 0), axis=1)
    block_number = jnp.arange(blocks_dev, dtype=jnp.int32)
    feature_part = block_number // group_blocks
    within_group = block_number % group_blocks
    source_block = (
        feature_part * group_blocks
        + inverse[within_group // owner_blocks] * owner_blocks
        + within_group % owner_blocks
    ).astype(jnp.int32)
    slots_t = jnp.swapaxes(bag_slots.reshape(blocks_dev, 128, bag_len), 1, 2)
    ids = block_ids.reshape(blocks_dev * list_len).astype(jnp.int32)
    counts = bag_counts.reshape(blocks_dev).astype(jnp.int32)
    gathered = lax.all_gather(hot_rows, "cache", axis=0, tiled=True)
    pooled = pool(source_block, ids, counts, slots_t, gathered, table)
    pooled = pooled.reshape(feat_dev, caches, samp_dev, row_width)
    features = lax.all_to_all(pooled, "cache", split_axis=1, concat_axis=0, tiled=True)[:, 0]
    products = jnp.einsum("fne,gne->nfg", features, features, preferred_element_type=jnp.float32)
    interaction = (products / math.sqrt(row_width)).astype(jnp.bfloat16)
    flat_rows = interaction.reshape(interaction.shape[0], -1)
    pre_norm = jnp.dot(flat_rows, top_weight, preferred_element_type=jnp.float32)
    sample_count = pre_norm.shape[0] * lax.axis_size("shard") * caches
    col_mean = lax.psum(jnp.sum(pre_norm, axis=0), ("shard", "cache")) / sample_count
    centered = pre_norm - col_mean
    col_var = lax.psum(jnp.sum(centered * centered, axis=0), ("shard", "cache")) / sample_count
    normed = (pre_norm - col_mean) * lax.rsqrt(col_var + norm_eps) * bn_gain + bn_shift
    top_hidden = jax.nn.relu(normed).astype(jnp.bfloat16)
    logits = jnp.dot(top_hidden, out_weight, preferred_element_type=jnp.float32)
    return (top_hidden, logits)


def solution(mesh):
    return jax.shard_map(
        shards,
        mesh=mesh,
        in_specs=(
            P(("shard", "cache"), None),
            P(("shard", "cache")),
            P("cache", "shard", None),
            P("cache", "shard", None),
            P("cache", "shard"),
            P("shard"),
            P(),
            P(),
            P(),
            P(),
        ),
        out_specs=(P(("shard", "cache"), None), P(("shard", "cache"))),
        check_vma=False,
    )
```

time: 629 us -> 452 us (0.72)
  other arithmetic: 157 us -> 2.71 us
  local copies, waits for them, and re-layouts: 92.6 us -> 8.81 us
  starting transfers between devices: 4.59 us -> 71.7 us
  matrix products: 49.1 us -> 3.8 us
  Pallas kernels: 0 us -> 19.1 us
  blocking collectives: 213 us -> 231 us
    reduce_sum x8 -> x0, other arithmetic: 149 us -> none  [one_batch(): jnp.sum((slots[..., None] == lane_ids).astype(jnp.float32), axis=2)]
    all_to_all x1, starting transfers between devices: 4.55 us -> 71.6 us  [shards(): lax.all_to_all(pooled, 'cache', split_axis=1, concat_axis=0, tiled=True)]
    dot_general x8 -> x0, matrix products: 45.3 us -> none  [one_batch(): jnp.einsum('bskr,bkre->bse', matches, panel_rows, preferred_element_type=...]
    reduce_sum x8 -> x0, local copies, waits for them, and re-layouts: 42.8 us -> none  [one_batch(): jnp.sum((slots[..., None] == lane_ids).astype(jnp.float32), axis=2)]
    gather x12 -> x0, local copies, waits for them, and re-layouts: 41.2 us -> none  [the longest x8 38.6 us: one_batch(): panel_rows = jnp.take(source, picks, axis=0)]
    pallas_call x0 -> x1, Pallas kernels: none -> 19.1 us  [pool(): pl.pallas_call(pool_kernel, grid_spec=grid_spec, out_shape=jax.ShapeDtype...]
    psum x1, blocking collectives: 108 us -> 123 us  [shards(): lax.psum(jnp.sum(pre_norm, axis=0), ('shard', 'cache')) / sample_count]
where the time goes in v1:
time: 452 us; the launch traced here: 450 us
  blocking collectives  231 us (51%)
  waiting for transfers between devices  98.9 us (22%)
  starting transfers between devices  71.7 us (16%)
  Pallas kernels  19.1 us (4%)
  between operations  14.2 us (3%)
  local copies, waits for them, and re-layouts  8.81 us (2%)
    psum x1, blocking collectives, shards(): lax.psum(jnp.sum(pre_norm, axis=0), ('shard', 'cache')) / sample_count  123 us
    psum x1, blocking collectives, shards(): lax.psum(jnp.sum(centered * centered, axis=0), ('shard', 'cache'))  108 us
    all_to_all x1, starting transfers between devices, shards(): lax.all_to_all(pooled, 'cache', split_axis=1, concat_axis=0, tiled=True)  71.6 us
    all_gather x1, waiting for transfers between devices, shards(): gathered = lax.all_gather(hot_rows, 'cache', axis=0, tiled=True)  49.7 us
    all_to_all x1, waiting for transfers between devices, shards(): lax.all_to_all(pooled, 'cache', split_axis=1, concat_axis=0, tiled=True)  49.2 us
    pallas_call x1, Pallas kernels, pool(): pl.pallas_call(pool_kernel, grid_spec=grid_spec, out_shape=jax.ShapeDtype...  19.1 us
  transfers between devices with their start and end apart: 2, of which 2 were waited for; matrix products, arithmetic and copies ran while one was open for 1% of the time, Pallas kernels for 0%

profile of v1, /device:TPU:6, one launch (start us, length us, event | category | flops | bytes accessed | tf_op | source)
XLA Modules:
  0.0 449.7 jit_solution(9834314894545838424)
XLA Ops:
  7.2 0.0 copy-start
  7.2 0.0 copy-start.2
  7.2 0.0 copy-start.8
  7.2 0.0 all-gather.2.cloned.1.call-start
  7.3 0.7 compare_select_fusion
  8.0 0.7 compare_and_fusion
  8.7 0.1 broadcast_bitcast_fusion
  8.7 1.6 gather_fusion.1
  10.3 0.8 bitcast_select_fusion
  11.1 0.0 all-gather.2.cloned.1.call-update
  11.2 1.0 copy.32
  12.2 0.2 copy.38
  12.3 0.8 copy.27
  13.1 0.1 reshape.115.ids_ref
  13.2 0.1 select_reduce_fusion
  13.3 0.7 gather_fusion
  14.0 49.7 %all-gather.2.cloned.1.call-done.hot_ref = bf16[6144,256]{1,0:T(8,128)(2,1)} async-done(((bf16[384,256]{1,0:T(8,128)(2,1)}), bf16[6144,256]{1,0:T(8,128)(2,1)}) %all-gather.2.cloned.1.call-update) | async-done | bytes 3145744 | tf_op jit(solution)/shard_map/all_gather | solution.py:109
  63.7 1.9 copy-done.1
  65.6 19.1 %shard_map.113 = bf16[4096,256]{1,0:T(8,128)(2,1)} custom-call(s32[32]{0:T(128)S(1)} %fusion.3.order_ref, s32[512]{0:T(512)S(1)} %reshape.115.ids_ref, s32[32]{0:T(128)S(1)} %bitcast.30, s32[32,16,128]{2,1,0:T(8,128)S(1)} %bitcast.28, bf16[6144,256]{1,0:T(8,128)(2,1)S(1)} %copy-done.1, bf16[1024,256]{1,0:T(8,128)(2,1)S(1)} %copy-done.2), custom_call_target="tpu_custom_call" | custom-call | tf_op jit(solution)/shard_map/pallas_call | solution.py:64
  84.7 71.6 %all-to-all-start = ((bf16[1,16,256,256]{3,2,0,1:T(8,128)(2,1)}), bf16[1,16,256,256]{3,2,0,1:T(8,128)(2,1)S(1)}, u32[]{:S(2)}, u32[]{:S(2)}) async-start(bf16[1,16,256,256]{3,2,0,1:T(8,128)(2,1)} %bitcast.7), calls=%async_computation | async-start | bytes 4194304 | tf_op jit(solution)/shard_map/all_to_all | solution.py:112
  156.4 49.2 %all-to-all-done = bf16[1,16,256,256]{3,2,0,1:T(8,128)(2,1)S(1)} async-done(((bf16[1,16,256,256]{3,2,0,1:T(8,128)(2,1)}), bf16[1,16,256,256]{3,2,0,1:T(8,128)(2,1)S(1)}, u32[]{:S(2)}, u32[]{:S(2)}) %all-to-all-start) | async-done | bytes 2097184 | tf_op jit(solution)/shard_map/all_to_all | solution.py:112
  205.6 2.7 fusion
  208.3 2.5 copy.31
  210.8 0.3 fusion.8
  211.1 122.8 %psum.14 = f32[1024]{0:T(1024)S(1)} all-reduce(f32[1024]{0:T(1024)S(1)} %get-tuple-element.2), channel_id=1, replica_groups=mesh['shard'=48,'cache'=16] {'shard','cache'}, use_global_device_ids=true, to_apply=%region_2.3 | all-reduce | flops 1024 | bytes 8192 | tf_op jit(solution)/shard_map/psum | solution.py:118
  334.0 0.1 multiply_reduce_fusion
  334.1 107.7 %psum.15 = f32[1024]{0:T(1024)S(1)} all-reduce(f32[1024]{0:T(1024)S(1)} %multiply_reduce_fusion), channel_id=1, replica_groups=mesh['shard'=48,'cache'=16] {'shard','cache'}, use_global_device_ids=true, to_apply=%region_4.5 | all-reduce | flops 1024 | bytes 8192 | tf_op jit(solution)/shard_map/psum | solution.py:120
  441.8 0.0 copy-done.6
  441.8 0.2 maximum_convert_fusion
  442.1 0.0 copy-start.4
  442.1 0.8 fusion.9
  442.9 0.0 copy-done.4
  (19 shorter events, 0.1 us)
Async XLA Ops:
  7.2 203.6 %copy-start = (bf16[256,1024]{1,0:T(8,128)(2,1)S(1)}, bf16[256,1024]{1,0:T(8,128)(2,1)}, u32[]{:S(2)}) copy-start(bf16[256,1024]{1,0:T(8,128)(2,1)} %param.16) | copy-start | bytes 1572868
  7.2 56.6 %copy-start.2 = (bf16[1024,256]{1,0:T(8,128)(2,1)S(1)}, bf16[1024,256]{1,0:T(8,128)(2,1)}, u32[]{:S(2)}) copy-start(bf16[1024,256]{1,0:T(8,128)(2,1)} %own_ref.1) | copy-start | bytes 1572868
  7.2 6.0 %copy-start.8 = (s32[16]{0:T(128)S(1)}, s32[16]{0:T(128)}, u32[]{:S(2)}) copy-start(s32[16]{0:T(128)} %param.15) | copy-start | bytes 196
  7.2 56.5 %copy-start.3 = (s32[1,32]{1,0:T(1,128)S(1)}, s32[1,32]{1,0:T(1,128)}, u32[]{:S(2)}) copy-start(s32[1,32]{1,0:T(1,128)} %param.14) | copy-start | bytes 388
  7.2 56.5 %all-gather.2.cloned.1.call-start = ((), (), s32[]{:S(2)}) async-start(), calls=%async_computation.1 | async-start | bytes 3342336 | tf_op jit(solution)/shard_map/all_gather | solution.py:109
  63.7 1.9 copy-start.1
  84.7 71.7 %copy-start.7 = (bf16[1024]{0:T(1024)(128)(2,1)S(1)}, bf16[1024]{0:T(1024)(128)(2,1)}, u32[]{:S(2)}) copy-start(bf16[1024]{0:T(1024)(128)(2,1)} %param.19) | copy-start | bytes 6148
  84.7 120.9 %all-to-all-start = ((bf16[1,16,256,256]{3,2,0,1:T(8,128)(2,1)}), bf16[1,16,256,256]{3,2,0,1:T(8,128)(2,1)S(1)}, u32[]{:S(2)}, u32[]{:S(2)}) async-start(bf16[1,16,256,256]{3,2,0,1:T(8,128)(2,1)} %bitcast.7), calls=%async_computation | async-start | bytes 4194304 | tf_op jit(solution)/shard_map/all_to_all | solution.py:112
  210.7 231.1 %copy-start.5 = (f32[1024]{0:T(1024)S(1)}, f32[1024]{0:T(1024)}, u32[]{:S(2)}) copy-start(f32[1024]{0:T(1024)} %param.18) | copy-start | bytes 12292
  210.8 231.1 %copy-start.6 = (f32[1024]{0:T(1024)S(1)}, f32[1024]{0:T(1024)}, u32[]{:S(2)}) copy-start(f32[1024]{0:T(1024)} %param.17) | copy-start | bytes 12292
  442.1 0.8 copy-start.4
Sparse Core Ops, SparseCore 0:
  11.3 52.4 all-gather.1

commit v2 on v1

--- a/solution.py
+++ b/solution.py
@@ -71,6 +71,50 @@
     )(order, ids, counts, slots_t, hot, own)
 
 
+def merge_pair(stats, axis, size, bit, count):
+    mean, m2 = stats[0], stats[1]
+    other = lax.ppermute(stats, axis, [(i, i ^ bit) for i in range(size)])
+    gap = mean - other[0]
+    merged_mean = (mean + other[0]) * 0.5
+    merged_m2 = (m2 + other[1]) + gap * gap * (count * 0.5)
+    return jnp.stack([merged_mean, merged_m2])
+
+
+def merge_three(stats, axis, size, stride, count):
+    place = lax.axis_index(axis) // stride
+    back = lax.ppermute(stats, axis, [(i, (i + stride) % size) for i in range(size)])
+    ahead = lax.ppermute(stats, axis, [(i, (i + 2 * stride) % size) for i in range(size)])
+    parts = []
+    for pos in range(3):
+        parts.append(
+            jnp.where(place == pos, stats, jnp.where((place + 2) % 3 == pos, back, ahead))
+        )
+    mean = (parts[0][0] + parts[1][0] + parts[2][0]) / 3.0
+    m2 = parts[0][1] + parts[1][1] + parts[2][1]
+    spread = (parts[0][0] - mean) ** 2 + (parts[1][0] - mean) ** 2 + (parts[2][0] - mean) ** 2
+    return jnp.stack([mean, m2 + spread * count])
+
+
+def column_stats(values, axes):
+    count = float(values.shape[0])
+    mean = jnp.sum(values, axis=0) / count
+    centered = values - mean
+    stats = jnp.stack([mean, jnp.sum(centered * centered, axis=0)])
+    for axis, size in axes:
+        bit = 1
+        while size % (2 * bit) == 0:
+            stats = merge_pair(stats, axis, size, bit, count)
+            count *= 2
+            bit *= 2
+        rest = size // bit
+        if rest == 3:
+            stats = merge_three(stats, axis, size, bit, count)
+            count *= 3
+        elif rest != 1:
+            raise ValueError("axis size")
+    return stats[0], stats[1]
+
+
 def shards(
     table,
     panel_ids,
@@ -114,10 +158,8 @@
     interaction = (products / math.sqrt(row_width)).astype(jnp.bfloat16)
     flat_rows = interaction.reshape(interaction.shape[0], -1)
     pre_norm = jnp.dot(flat_rows, top_weight, preferred_element_type=jnp.float32)
-    sample_count = pre_norm.shape[0] * lax.axis_size("shard") * caches
-    col_mean = lax.psum(jnp.sum(pre_norm, axis=0), ("shard", "cache")) / sample_count
-    centered = pre_norm - col_mean
-    col_var = lax.psum(jnp.sum(centered * centered, axis=0), ("shard", "cache")) / sample_count
+    col_mean, col_m2 = column_stats(pre_norm, (("cache", caches), ("shard", lax.axis_size("shard"))))
+    col_var = col_m2 / (pre_norm.shape[0] * lax.axis_size("shard") * caches)
     normed = (pre_norm - col_mean) * lax.rsqrt(col_var + norm_eps) * bn_gain + bn_shift
     top_hidden = jax.nn.relu(normed).astype(jnp.bfloat16)
     logits = jnp.dot(top_hidden, out_weight, preferred_element_type=jnp.float32)

time: 452 us -> 298 us (0.66)
  blocking collectives: 231 us -> 126 us
  starting transfers between devices: 71.7 us -> 46.5 us
  waiting for transfers between devices: 98.9 us -> 82.1 us
    psum x2 -> x0, blocking collectives: 231 us -> none  [the longest x1 123 us: shards(): lax.psum(jnp.sum(pre_norm, axis=0), ('shard', 'cache')) / sample_count]
    all_to_all x0 -> x1, blocking collectives: none -> 126 us  [shards(): lax.all_to_all(pooled, 'cache', split_axis=1, concat_axis=0, tiled=True)]
    all_to_all x1 -> x0, starting transfers between devices: 71.6 us -> none  [shards(): lax.all_to_all(pooled, 'cache', split_axis=1, concat_axis=0, tiled=True)]
    all_to_all x1 -> x0, waiting for transfers between devices: 49.2 us -> none  [shards(): lax.all_to_all(pooled, 'cache', split_axis=1, concat_axis=0, tiled=True)]
    ppermute x0 -> x10, starting transfers between devices: none -> 46.4 us  [the longest x8 36.7 us: merge_pair(): other = lax.ppermute(stats, axis, [(i, i ^ bit) for i in range(size)])]
    ppermute x0 -> x10, waiting for transfers between devices: none -> 32.4 us  [the longest x8 26.5 us: merge_pair(): other = lax.ppermute(stats, axis, [(i, i ^ bit) for i in range(size)])]
  transfers between devices with their start and end apart: 2 -> 11, of which waited for: 2 -> 10; matrix products, arithmetic and copies ran while one was open for 1% -> 1% of each run, Pallas kernels for 0% -> 0%
where the time goes in v2:
time: 298 us; the launch traced here: 297 us
  blocking collectives  126 us (42%)
  waiting for transfers between devices  82.1 us (28%)
  starting transfers between devices  46.5 us (16%)
  Pallas kernels  15.8 us (5%)
  between operations  14.4 us (5%)
  local copies, waits for them, and re-layouts  7.34 us (2%)
  other arithmetic  2.99 us (1%)
    all_to_all x1, blocking collectives, shards(): lax.all_to_all(pooled, 'cache', split_axis=1, concat_axis=0, tiled=True)  126 us
    all_gather x1, waiting for transfers between devices, shards(): gathered = lax.all_gather(hot_rows, 'cache', axis=0, tiled=True)  49.7 us
    ppermute x8, starting transfers between devices, merge_pair(): other = lax.ppermute(stats, axis, [(i, i ^ bit) for i in range(size)])  36.7 us
    ppermute x8, waiting for transfers between devices, merge_pair(): other = lax.ppermute(stats, axis, [(i, i ^ bit) for i in range(size)])  26.5 us
    pallas_call x1, Pallas kernels, pool(): pl.pallas_call(pool_kernel, grid_spec=grid_spec, out_shape=jax.ShapeDtype...  15.8 us
    ppermute x1, starting transfers between devices, merge_three(): lax.ppermute(stats, axis, [(i, (i + stride) % size) for i in range(size)])  6.29 us
  transfers between devices with their start and end apart: 11, of which 10 were waited for; matrix products, arithmetic and copies ran while one was open for 1% of the time, Pallas kernels for 0%

profile of v2, /device:TPU:6, one launch (start us, length us, event | category | flops | bytes accessed | tf_op | source)
XLA Modules:
  0.0 297.1 jit_solution(4168907563406160536)
XLA Ops:
  7.3 0.7 compare_select_fusion
  8.7 1.6 gather_fusion.1
  10.3 0.8 bitcast_select_fusion
  11.2 1.0 copy.32
  12.3 0.8 copy.27
  13.3 0.7 gather_fusion
  14.0 49.7 %all-gather.2.cloned.1.call-done.hot_ref = bf16[6144,256]{1,0:T(8,128)(2,1)} async-done(((bf16[384,256]{1,0:T(8,128)(2,1)}), bf16[6144,256]{1,0:T(8,128)(2,1)}) %all-gather.2.cloned.1.call-update) | async-done | bytes 3145744 | tf_op jit(solution)/shard_map/all_gather | solution.py:153
  63.7 1.9 copy-done.1
  65.6 15.8 %shard_map.113 = bf16[4096,256]{1,0:T(8,128)(2,1)S(1)} custom-call(s32[32]{0:T(128)S(1)} %fusion.12.order_ref, s32[512]{0:T(512)S(1)} %reshape.146.ids_ref, s32[32]{0:T(128)S(1)} %bitcast.35, s32[32,16,128]{2,1,0:T(8,128)S(1)} %bitcast.33, bf16[6144,256]{1,0:T(8,128)(2,1)S(1)} %copy-done.1, bf16[1024,256]{1,0:T(8,128)(2,1)S(1)} %copy-done.2), custom_call_target="tpu_custom_call" | custom-call | tf_op jit(solution)/shard_map/pallas_call | solution.py:64
  81.4 125.6 %all_to_all.4 = bf16[1,16,256,256]{3,2,0,1:T(8,128)(2,1)S(1)} all-to-all(bf16[1,16,256,256]{3,2,0,1:T(8,128)(2,1)S(1)} %bitcast.32), channel_id=1, replica_groups=mesh['shard'=48,'cache'=16] {'cache'}, dimensions={1} | all-to-all | bytes 4194304 | tf_op jit(solution)/shard_map/all_to_all | solution.py:156
  207.0 1.3 fusion
  208.3 1.0 copy.31
  209.9 3.6 %collective-permute-start = (f32[2,1024]{1,0:T(2,128)S(1)}, f32[2,1024]{1,0:T(2,128)S(1)}, u32[]{:S(2)}, u32[]{:S(2)}) collective-permute-start(f32[2,1024]{1,0:T(2,128)S(1)} %pad_maximum_fusion), channel_id=1, source_target_pairs={{0,1},{1,0},{2,3},{3,2},{4,5},{5,4},{6,7},{7,6},{8,9},{9,8},{10,11... | collective-permute-start | bytes 24584 | tf_op jit(solution)/shard_map/ppermute | solution.py:76
  213.5 0.8 collective-permute-done
  214.3 1.9 collective-permute-start.1
  216.2 3.6 %collective-permute-done.1 = f32[2,1024]{1,0:T(2,128)S(1)} collective-permute-done((f32[2,1024]{1,0:T(2,128)S(1)}, f32[2,1024]{1,0:T(2,128)S(1)}, u32[]{:S(2)}, u32[]{:S(2)}) %collective-permute-start.1) | collective-permute-done | bytes 8224 | tf_op jit(solution)/shard_map/ppermute | solution.py:76
  219.9 2.4 collective-permute-start.2
  222.3 4.1 %collective-permute-done.2 = f32[2,1024]{1,0:T(2,128)S(1)} collective-permute-done((f32[2,1024]{1,0:T(2,128)S(1)}, f32[2,1024]{1,0:T(2,128)S(1)}, u32[]{:S(2)}, u32[]{:S(2)}) %collective-permute-start.2) | collective-permute-done | bytes 8224 | tf_op jit(solution)/shard_map/ppermute | solution.py:76
  226.4 3.4 %collective-permute-start.3 = (f32[2,1024]{1,0:T(2,128)S(1)}, f32[2,1024]{1,0:T(2,128)S(1)}, u32[]{:S(2)}, u32[]{:S(2)}) collective-permute-start(f32[2,1024]{1,0:T(2,128)S(1)} %pad_maximum_fusion.3), channel_id=1, source_target_pairs={{0,8},{1,9},{2,10},{3,11},{4,12},{5,13},{6,14},{7,15},{8,0},{9,1},... | collective-permute-start | bytes 24584 | tf_op jit(solution)/shard_map/ppermute | solution.py:76
  229.8 6.0 %collective-permute-done.3 = f32[2,1024]{1,0:T(2,128)S(1)} collective-permute-done((f32[2,1024]{1,0:T(2,128)S(1)}, f32[2,1024]{1,0:T(2,128)S(1)}, u32[]{:S(2)}, u32[]{:S(2)}) %collective-permute-start.3) | collective-permute-done | bytes 8224 | tf_op jit(solution)/shard_map/ppermute | solution.py:76
  235.9 12.8 %collective-permute-start.4 = (f32[2,1024]{1,0:T(2,128)S(1)}, f32[2,1024]{1,0:T(2,128)S(1)}, u32[]{:S(2)}, u32[]{:S(2)}) collective-permute-start(f32[2,1024]{1,0:T(2,128)S(1)} %pad_maximum_fusion.4), channel_id=1, source_target_pairs={{0,16},{16,0},{32,48},{48,32},{64,80},{80,64},{96,112},{112,96},{1... | collective-permute-start | bytes 24584 | tf_op jit(solution)/shard_map/ppermute | solution.py:76
  248.7 1.6 collective-permute-done.4
  250.3 1.9 collective-permute-start.5
  252.2 5.1 %collective-permute-done.5 = f32[2,1024]{1,0:T(2,128)S(1)} collective-permute-done((f32[2,1024]{1,0:T(2,128)S(1)}, f32[2,1024]{1,0:T(2,128)S(1)}, u32[]{:S(2)}, u32[]{:S(2)}) %collective-permute-start.5) | collective-permute-done | bytes 8224 | tf_op jit(solution)/shard_map/ppermute | solution.py:76
  257.4 1.9 collective-permute-start.6
  259.3 3.6 %collective-permute-done.6 = f32[2,1024]{1,0:T(2,128)S(1)} collective-permute-done((f32[2,1024]{1,0:T(2,128)S(1)}, f32[2,1024]{1,0:T(2,128)S(1)}, u32[]{:S(2)}, u32[]{:S(2)}) %collective-permute-start.6) | collective-permute-done | bytes 8224 | tf_op jit(solution)/shard_map/ppermute | solution.py:76
  263.0 8.8 %collective-permute-start.7 = (f32[2,1024]{1,0:T(2,128)S(1)}, f32[2,1024]{1,0:T(2,128)S(1)}, u32[]{:S(2)}, u32[]{:S(2)}) collective-permute-start(f32[2,1024]{1,0:T(2,128)S(1)} %pad_maximum_fusion.7), channel_id=1, source_target_pairs={{0,128},{16,144},{32,160},{48,176},{64,192},{80,208},{96,224},{112... | collective-permute-start | bytes 24584 | tf_op jit(solution)/shard_map/ppermute | solution.py:76
  271.7 1.6 collective-permute-done.7
  273.4 6.3 %collective-permute-start.8 = (f32[2,1024]{1,0:T(2,128)S(1)}, f32[2,1024]{1,0:T(2,128)S(1)}, u32[]{:S(2)}, u32[]{:S(2)}) collective-permute-start(f32[2,1024]{1,0:T(2,128)S(1)} %pad_maximum_fusion.8), channel_id=1, source_target_pairs={{0,256},{16,272},{32,288},{48,304},{64,320},{80,336},{96,352},{112... | collective-permute-start | bytes 24584 | tf_op jit(solution)/shard_map/ppermute | solution.py:85
  279.7 3.5 %collective-permute-start.9 = (f32[2,1024]{1,0:T(2,128)S(1)}, f32[2,1024]{1,0:T(2,128)S(1)}, u32[]{:S(2)}, u32[]{:S(2)}) collective-permute-start(f32[2,1024]{1,0:T(2,128)S(1)} %pad_maximum_fusion.8), channel_id=1, source_target_pairs={{0,512},{16,528},{32,544},{48,560},{64,576},{80,592},{96,608},{112... | collective-permute-start | bytes 24584 | tf_op jit(solution)/shard_map/ppermute | solution.py:86
  283.2 5.9 %collective-permute-done.9 = f32[2,1024]{1,0:T(2,128)S(1)} collective-permute-done((f32[2,1024]{1,0:T(2,128)S(1)}, f32[2,1024]{1,0:T(2,128)S(1)}, u32[]{:S(2)}, u32[]{:S(2)}) %collective-permute-start.9) | collective-permute-done | bytes 8224 | tf_op jit(solution)/shard_map/ppermute | solution.py:86
  289.4 0.8 fusion.18
  (54 shorter events, 2.2 us)
Async XLA Ops:
  7.2 202.2 %copy-start = (bf16[256,1024]{1,0:T(8,128)(2,1)S(1)}, bf16[256,1024]{1,0:T(8,128)(2,1)}, u32[]{:S(2)}) copy-start(bf16[256,1024]{1,0:T(8,128)(2,1)} %param.16) | copy-start | bytes 1572868
  7.2 56.6 %copy-start.2 = (bf16[1024,256]{1,0:T(8,128)(2,1)S(1)}, bf16[1024,256]{1,0:T(8,128)(2,1)}, u32[]{:S(2)}) copy-start(bf16[1024,256]{1,0:T(8,128)(2,1)} %own_ref.1) | copy-start | bytes 1572868
  7.2 6.0 %copy-start.8 = (s32[16]{0:T(128)S(1)}, s32[16]{0:T(128)}, u32[]{:S(2)}) copy-start(s32[16]{0:T(128)} %param.15) | copy-start | bytes 196
  7.2 56.5 %copy-start.3 = (s32[1,32]{1,0:T(1,128)S(1)}, s32[1,32]{1,0:T(1,128)}, u32[]{:S(2)}) copy-start(s32[1,32]{1,0:T(1,128)} %param.14) | copy-start | bytes 388
  7.2 56.5 %all-gather.2.cloned.1.call-start = ((), (), s32[]{:S(2)}) async-start(), calls=%async_computation.1 | async-start | bytes 3342336 | tf_op jit(solution)/shard_map/all_gather | solution.py:153
  63.7 1.9 copy-start.1
  209.3 73.9 %copy-start.7 = (bf16[1024]{0:T(1024)(128)(2,1)S(1)}, bf16[1024]{0:T(1024)(128)(2,1)}, u32[]{:S(2)}) copy-start(bf16[1024]{0:T(1024)(128)(2,1)} %param.19) | copy-start | bytes 6148
  209.3 79.9 %copy-start.5 = (f32[1024]{0:T(1024)S(1)}, f32[1024]{0:T(1024)}, u32[]{:S(2)}) copy-start(f32[1024]{0:T(1024)} %param.18) | copy-start | bytes 12292
  209.3 79.9 %copy-start.6 = (f32[1024]{0:T(1024)S(1)}, f32[1024]{0:T(1024)}, u32[]{:S(2)}) copy-start(f32[1024]{0:T(1024)} %param.17) | copy-start | bytes 12292
  209.9 4.4 %collective-permute-start = (f32[2,1024]{1,0:T(2,128)S(1)}, f32[2,1024]{1,0:T(2,128)S(1)}, u32[]{:S(2)}, u32[]{:S(2)}) collective-permute-start(f32[2,1024]{1,0:T(2,128)S(1)} %pad_maximum_fusion), channel_id=1, source_target_pairs={{0,1},{1,0},{2,3},{3,2},{4,5},{5,4},{6,7},{7,6},{8,9},{9,8},{10,11... | collective-permute-start | bytes 24584 | tf_op jit(solution)/shard_map/ppermute | solution.py:76
  214.3 5.5 %collective-permute-start.1 = (f32[2,1024]{1,0:T(2,128)S(1)}, f32[2,1024]{1,0:T(2,128)S(1)}, u32[]{:S(2)}, u32[]{:S(2)}) collective-permute-start(f32[2,1024]{1,0:T(2,128)S(1)} %pad_maximum_fusion.1), channel_id=1, source_target_pairs={{0,2},{1,3},{2,0},{3,1},{4,6},{5,7},{6,4},{7,5},{8,10},{9,11},{10,... | collective-permute-start | bytes 24584 | tf_op jit(solution)/shard_map/ppermute | solution.py:76
  219.9 6.4 %collective-permute-start.2 = (f32[2,1024]{1,0:T(2,128)S(1)}, f32[2,1024]{1,0:T(2,128)S(1)}, u32[]{:S(2)}, u32[]{:S(2)}) collective-permute-start(f32[2,1024]{1,0:T(2,128)S(1)} %pad_maximum_fusion.2), channel_id=1, source_target_pairs={{0,4},{1,5},{2,6},{3,7},{4,0},{5,1},{6,2},{7,3},{8,12},{9,13},{10,... | collective-permute-start | bytes 24584 | tf_op jit(solution)/shard_map/ppermute | solution.py:76
  226.4 9.5 %collective-permute-start.3 = (f32[2,1024]{1,0:T(2,128)S(1)}, f32[2,1024]{1,0:T(2,128)S(1)}, u32[]{:S(2)}, u32[]{:S(2)}) collective-permute-start(f32[2,1024]{1,0:T(2,128)S(1)} %pad_maximum_fusion.3), channel_id=1, source_target_pairs={{0,8},{1,9},{2,10},{3,11},{4,12},{5,13},{6,14},{7,15},{8,0},{9,1},... | collective-permute-start | bytes 24584 | tf_op jit(solution)/shard_map/ppermute | solution.py:76
  235.9 14.4 %collective-permute-start.4 = (f32[2,1024]{1,0:T(2,128)S(1)}, f32[2,1024]{1,0:T(2,128)S(1)}, u32[]{:S(2)}, u32[]{:S(2)}) collective-permute-start(f32[2,1024]{1,0:T(2,128)S(1)} %pad_maximum_fusion.4), channel_id=1, source_target_pairs={{0,16},{16,0},{32,48},{48,32},{64,80},{80,64},{96,112},{112,96},{1... | collective-permute-start | bytes 24584 | tf_op jit(solution)/shard_map/ppermute | solution.py:76
  250.3 7.0 %collective-permute-start.5 = (f32[2,1024]{1,0:T(2,128)S(1)}, f32[2,1024]{1,0:T(2,128)S(1)}, u32[]{:S(2)}, u32[]{:S(2)}) collective-permute-start(f32[2,1024]{1,0:T(2,128)S(1)} %pad_maximum_fusion.5), channel_id=1, source_target_pairs={{0,32},{16,48},{32,0},{48,16},{64,96},{80,112},{96,64},{112,80},{1... | collective-permute-start | bytes 24584 | tf_op jit(solution)/shard_map/ppermute | solution.py:76
  257.4 5.5 %collective-permute-start.6 = (f32[2,1024]{1,0:T(2,128)S(1)}, f32[2,1024]{1,0:T(2,128)S(1)}, u32[]{:S(2)}, u32[]{:S(2)}) collective-permute-start(f32[2,1024]{1,0:T(2,128)S(1)} %pad_maximum_fusion.6), channel_id=1, source_target_pairs={{0,64},{16,80},{32,96},{48,112},{64,0},{80,16},{96,32},{112,48},{1... | collective-permute-start | bytes 24584 | tf_op jit(solution)/shard_map/ppermute | solution.py:76
  263.0 10.4 %collective-permute-start.7 = (f32[2,1024]{1,0:T(2,128)S(1)}, f32[2,1024]{1,0:T(2,128)S(1)}, u32[]{:S(2)}, u32[]{:S(2)}) collective-permute-start(f32[2,1024]{1,0:T(2,128)S(1)} %pad_maximum_fusion.7), channel_id=1, source_target_pairs={{0,128},{16,144},{32,160},{48,176},{64,192},{80,208},{96,224},{112... | collective-permute-start | bytes 24584 | tf_op jit(solution)/shard_map/ppermute | solution.py:76
  273.4 9.8 %collective-permute-start.8 = (f32[2,1024]{1,0:T(2,128)S(1)}, f32[2,1024]{1,0:T(2,128)S(1)}, u32[]{:S(2)}, u32[]{:S(2)}) collective-permute-start(f32[2,1024]{1,0:T(2,128)S(1)} %pad_maximum_fusion.8), channel_id=1, source_target_pairs={{0,256},{16,272},{32,288},{48,304},{64,320},{80,336},{96,352},{112... | collective-permute-start | bytes 24584 | tf_op jit(solution)/shard_map/ppermute | solution.py:85
  279.7 9.5 %collective-permute-start.9 = (f32[2,1024]{1,0:T(2,128)S(1)}, f32[2,1024]{1,0:T(2,128)S(1)}, u32[]{:S(2)}, u32[]{:S(2)}) collective-permute-start(f32[2,1024]{1,0:T(2,128)S(1)} %pad_maximum_fusion.8), channel_id=1, source_target_pairs={{0,512},{16,528},{32,544},{48,560},{64,576},{80,592},{96,608},{112... | collective-permute-start | bytes 24584 | tf_op jit(solution)/shard_map/ppermute | solution.py:86
  289.4 0.8 copy-start.4
Sparse Core Ops, SparseCore 0:
  11.3 52.4 all-gather.1

commit v3 on v2

--- a/solution.py
+++ b/solution.py
@@ -11,55 +11,71 @@
 norm_eps = 1e-05
 
 
-def pool_kernel(order_ref, ids_ref, counts_ref, slots_ref, hot_ref, own_ref, out_ref, acc_ref):
+def pool_kernel(order_ref, ids_ref, counts_ref, slots_ref, hot_ref, own_ref, out_ref, hits_ref, cols_ref):
     step = pl.program_id(0)
     block = order_ref[step]
     list_len = slots_ref.shape[1]
-    hot_count = hot_ref.shape[0] // 128
-    own_count = own_ref.shape[0] // 128
+    hot_devices, _, hot_width = hot_ref.shape
+    hot_dev = hot_width // 128
+    hot_count = hot_devices * hot_dev
+    own_count = own_ref.shape[1] // 128
     slots = slots_ref[0]
     row_iota = lax.broadcasted_iota(jnp.int32, (128, 128), 0)
-    acc_ref[...] = jnp.zeros(acc_ref.shape, jnp.float32)
+
+    @pl.when(step == 0)
+    def _():
+        cols_ref[...] = jnp.zeros(cols_ref.shape, cols_ref.dtype)
 
     def place(k, carry):
         shifted = slots - k * 128
         hits = jnp.zeros((128, 128), jnp.float32)
         for entry in range(list_len):
             hits = hits + (shifted[entry : entry + 1, :] == row_iota).astype(jnp.float32)
+        start = pl.multiple_of(k * 128, 128)
+        hits_ref[pl.ds(start, 128), :] = hits.astype(hits_ref.dtype)
         name = jnp.clip(ids_ref[block * list_len + k], 0, hot_count + own_count - 1)
-        hot_start = pl.multiple_of(jnp.minimum(name, hot_count - 1) * 128, 128)
+        hot_name = jnp.minimum(name, hot_count - 1)
+        hot_start = pl.multiple_of((hot_name % hot_dev) * 128, 128)
         own_start = pl.multiple_of(jnp.maximum(name - hot_count, 0) * 128, 128)
-        rows = jnp.where(
-            name < hot_count,
-            hot_ref[pl.ds(hot_start, 128), :],
-            own_ref[pl.ds(own_start, 128), :],
-        )
-        acc_ref[...] += lax.dot_general(
-            hits.astype(jnp.bfloat16),
-            rows,
-            (((0,), (0,)), ((), ())),
-            preferred_element_type=jnp.float32,
-        )
+
+        @pl.when(name < hot_count)
+        def _():
+            cols_ref[:, pl.ds(start, 128)] = hot_ref[hot_name // hot_dev, :, pl.ds(hot_start, 128)]
+
+        @pl.when(name >= hot_count)
+        def _():
+            cols_ref[:, pl.ds(start, 128)] = own_ref[:, pl.ds(own_start, 128)]
+
+        return carry
+
+    def unused(k, carry):
+        start = pl.multiple_of(k * 128, 128)
+        hits_ref[pl.ds(start, 128), :] = jnp.zeros((128, 128), hits_ref.dtype)
         return carry
 
     count = jnp.clip(counts_ref[block], 0, list_len)
     lax.fori_loop(0, count, place, 0)
-    out_ref[...] = acc_ref[...].astype(out_ref.dtype)
-
-
-def pool(order, ids, counts, slots_t, hot, own):
+    lax.fori_loop(count, list_len, unused, 0)
+    total = jnp.dot(cols_ref[...], hits_ref[...], preferred_element_type=jnp.float32)
+    out_ref[...] = total.T.astype(out_ref.dtype)
+
+
+def pool(order, ids, counts, slots_t, hot_t, own_t):
     blocks, bag_len, _ = slots_t.shape
-    width = hot.shape[1]
+    width = own_t.shape[0]
     grid_spec = pltpu.PrefetchScalarGridSpec(
         num_scalar_prefetch=3,
         grid=(blocks,),
         in_specs=[
             pl.BlockSpec((1, bag_len, 128), lambda i, o, d, c: (o[i], 0, 0)),
-            pl.BlockSpec(hot.shape, lambda i, o, d, c: (0, 0)),
-            pl.BlockSpec(own.shape, lambda i, o, d, c: (0, 0)),
+            pl.BlockSpec(hot_t.shape, lambda i, o, d, c: (0, 0, 0)),
+            pl.BlockSpec(own_t.shape, lambda i, o, d, c: (0, 0)),
         ],
         out_specs=pl.BlockSpec((128, width), lambda i, o, d, c: (i, 0)),
-        scratch_shapes=[pltpu.VMEM((128, width), jnp.float32)],
+        scratch_shapes=[
+            pltpu.VMEM((bag_len * 128, 128), jnp.bfloat16),
+            pltpu.VMEM((width, bag_len * 128), jnp.bfloat16),
+        ],
     )
     return pl.pallas_call(
         pool_kernel,
@@ -68,8 +84,7 @@
         compiler_params=pltpu.CompilerParams(
             dimension_semantics=("arbitrary",), vmem_limit_bytes=40 * 1024 * 1024
         ),
-    )(order, ids, counts, slots_t, hot, own)
-
+    )(order, ids, counts, slots_t, hot_t, own_t)
 
 def merge_pair(stats, axis, size, bit, count):
     mean, m2 = stats[0], stats[1]
@@ -150,8 +165,8 @@
     slots_t = jnp.swapaxes(bag_slots.reshape(blocks_dev, 128, bag_len), 1, 2)
     ids = block_ids.reshape(blocks_dev * list_len).astype(jnp.int32)
     counts = bag_counts.reshape(blocks_dev).astype(jnp.int32)
-    gathered = lax.all_gather(hot_rows, "cache", axis=0, tiled=True)
-    pooled = pool(source_block, ids, counts, slots_t, gathered, table)
+    gathered = lax.all_gather(hot_rows.T, "cache", axis=0)
+    pooled = pool(source_block, ids, counts, slots_t, gathered, table.T)
     pooled = pooled.reshape(feat_dev, caches, samp_dev, row_width)
     features = lax.all_to_all(pooled, "cache", split_axis=1, concat_axis=0, tiled=True)[:, 0]
     products = jnp.einsum("fne,gne->nfg", features, features, preferred_element_type=jnp.float32)

time: 298 us -> 269 us (0.903)
  blocking collectives: 126 us -> 73.9 us
  Pallas kernels: 15.8 us -> 37.6 us
  starting transfers between devices: 46.5 us -> 39.8 us
  local copies, waits for them, and re-layouts: 7.34 us -> 11.6 us
  waiting for transfers between devices: 82.1 us -> 85.3 us
    all_to_all x1, blocking collectives: 126 us -> 73.9 us  [shards(): lax.all_to_all(pooled, 'cache', split_axis=1, concat_axis=0, tiled=True)]
    pallas_call x1, Pallas kernels: 15.8 us -> 37.6 us  [pool(): pl.pallas_call(pool_kernel, grid_spec=grid_spec, out_shape=jax.ShapeDtype...]
    ppermute x8, starting transfers between devices: 36.7 us -> 28 us  [merge_pair(): other = lax.ppermute(stats, axis, [(i, i ^ bit) for i in range(size)])]
    all_gather x0 -> x1, local copies, waits for them, and re-layouts: none -> 4.65 us  [shards(): gathered = lax.all_gather(hot_rows.T, 'cache', axis=0)]
    all_gather x1, waiting for transfers between devices: 49.7 us -> 54 us  [shards(): gathered = lax.all_gather(hot_rows.T, 'cache', axis=0)]
where the time goes in v3:
time: 269 us; the launch traced here: 268 us
  waiting for transfers between devices  85.3 us (32%)
  blocking collectives  73.9 us (27%)
  starting transfers between devices  39.8 us (15%)
  Pallas kernels  37.6 us (14%)
  between operations  14.5 us (5%)
  local copies, waits for them, and re-layouts  11.6 us (4%)
  other arithmetic  2.97 us (1%)
    all_to_all x1, blocking collectives, shards(): lax.all_to_all(pooled, 'cache', split_axis=1, concat_axis=0, tiled=True)  73.9 us
    all_gather x1, waiting for transfers between devices, shards(): gathered = lax.all_gather(hot_rows.T, 'cache', axis=0)  54 us
    pallas_call x1, Pallas kernels, pool(): pl.pallas_call(pool_kernel, grid_spec=grid_spec, out_shape=jax.ShapeDtype...  37.6 us
    ppermute x8, starting transfers between devices, merge_pair(): other = lax.ppermute(stats, axis, [(i, i ^ bit) for i in range(size)])  28 us
    ppermute x8, waiting for transfers between devices, merge_pair(): other = lax.ppermute(stats, axis, [(i, i ^ bit) for i in range(size)])  25.9 us
    ppermute x1, starting transfers between devices, merge_three(): lax.ppermute(stats, axis, [(i, (i + stride) % size) for i in range(size)])  7.75 us
  transfers between devices with their start and end apart: 11, of which 10 were waited for; matrix products, arithmetic and copies ran while one was open for 1% of the time, Pallas kernels for 0%

profile of v3, /device:TPU:6, one launch (start us, length us, event | category | flops | bytes accessed | tf_op | source)
XLA Modules:
  0.0 268.1 jit_solution(2251632654056089758)
XLA Ops:
  7.3 0.7 compare_select_fusion
  8.7 1.6 gather_fusion.1
  10.3 0.8 bitcast_select_fusion
  11.1 1.2 copy.38
  13.0 0.7 gather_fusion
  13.7 54.0 %all-gather.3.cloned.1.call-done = bf16[4096,384]{0,1:T(8,128)(2,1)} async-done(((bf16[256,384]{0,1:T(8,128)(2,1)}), bf16[4096,384]{0,1:T(8,128)(2,1)}) %all-gather.3.cloned.1.call-update) | async-done | bytes 3145744 | tf_op jit(solution)/shard_map/all_gather | solution.py:168
  67.6 4.7 %copy.37 = bf16[4096,384]{1,0:T(8,128)(2,1)} copy(bf16[4096,384]{0,1:T(8,128)(2,1)} %all-gather.3.cloned.1.call-done) | data formatting | bytes 6291456 | tf_op jit(solution)/shard_map/all_gather | solution.py:168
  72.3 1.9 copy-done.1
  74.2 37.6 %shard_map.113 = bf16[4096,256]{1,0:T(8,128)(2,1)S(1)} custom-call(s32[32]{0:T(128)S(1)} %fusion.12.order_ref, s32[512]{0:T(512)S(1)} %reshape.146.ids_ref, s32[32]{0:T(128)S(1)} %bitcast.39, s32[32,16,128]{2,1,0:T(8,128)S(1)} %bitcast.38, bf16[16,256,384]{2,1,0:T(8,128)(2,1)S(1)} %bitcast.35, bf16[256,1024]{1,0:T(8,128)(2,1)S(1)} %bitcast.37), custom_call_target="tpu_custom_call" | custom-call | tf_op jit(solution)/shard_map/pallas_call | solution.py:80
  111.8 73.9 %all_to_all.4 = bf16[1,16,256,256]{3,2,0,1:T(8,128)(2,1)S(1)} all-to-all(bf16[1,16,256,256]{3,2,0,1:T(8,128)(2,1)S(1)} %bitcast.36), channel_id=1, replica_groups=mesh['shard'=48,'cache'=16] {'cache'}, dimensions={1} | all-to-all | bytes 4194304 | tf_op jit(solution)/shard_map/all_to_all | solution.py:171
  185.7 1.3 fusion
  187.0 1.0 copy.41
  188.6 3.6 %collective-permute-start = (f32[2,1024]{1,0:T(2,128)S(1)}, f32[2,1024]{1,0:T(2,128)S(1)}, u32[]{:S(2)}, u32[]{:S(2)}) collective-permute-start(f32[2,1024]{1,0:T(2,128)S(1)} %pad_maximum_fusion), channel_id=1, source_target_pairs={{0,1},{1,0},{2,3},{3,2},{4,5},{5,4},{6,7},{7,6},{8,9},{9,8},{10,11... | collective-permute-start | bytes 24584 | tf_op jit(solution)/shard_map/ppermute | solution.py:91
  192.2 0.8 collective-permute-done
  193.0 1.9 collective-permute-start.1
  194.9 3.6 %collective-permute-done.1 = f32[2,1024]{1,0:T(2,128)S(1)} collective-permute-done((f32[2,1024]{1,0:T(2,128)S(1)}, f32[2,1024]{1,0:T(2,128)S(1)}, u32[]{:S(2)}, u32[]{:S(2)}) %collective-permute-start.1) | collective-permute-done | bytes 8224 | tf_op jit(solution)/shard_map/ppermute | solution.py:91
  198.6 2.4 collective-permute-start.2
  201.0 4.1 %collective-permute-done.2 = f32[2,1024]{1,0:T(2,128)S(1)} collective-permute-done((f32[2,1024]{1,0:T(2,128)S(1)}, f32[2,1024]{1,0:T(2,128)S(1)}, u32[]{:S(2)}, u32[]{:S(2)}) %collective-permute-start.2) | collective-permute-done | bytes 8224 | tf_op jit(solution)/shard_map/ppermute | solution.py:91
  205.1 3.4 %collective-permute-start.3 = (f32[2,1024]{1,0:T(2,128)S(1)}, f32[2,1024]{1,0:T(2,128)S(1)}, u32[]{:S(2)}, u32[]{:S(2)}) collective-permute-start(f32[2,1024]{1,0:T(2,128)S(1)} %pad_maximum_fusion.3), channel_id=1, source_target_pairs={{0,8},{1,9},{2,10},{3,11},{4,12},{5,13},{6,14},{7,15},{8,0},{9,1},... | collective-permute-start | bytes 24584 | tf_op jit(solution)/shard_map/ppermute | solution.py:91
  208.5 6.0 %collective-permute-done.3 = f32[2,1024]{1,0:T(2,128)S(1)} collective-permute-done((f32[2,1024]{1,0:T(2,128)S(1)}, f32[2,1024]{1,0:T(2,128)S(1)}, u32[]{:S(2)}, u32[]{:S(2)}) %collective-permute-start.3) | collective-permute-done | bytes 8224 | tf_op jit(solution)/shard_map/ppermute | solution.py:91
  214.6 1.9 collective-permute-start.4
  216.5 3.6 %collective-permute-done.4 = f32[2,1024]{1,0:T(2,128)S(1)} collective-permute-done((f32[2,1024]{1,0:T(2,128)S(1)}, f32[2,1024]{1,0:T(2,128)S(1)}, u32[]{:S(2)}, u32[]{:S(2)}) %collective-permute-start.4) | collective-permute-done | bytes 8224 | tf_op jit(solution)/shard_map/ppermute | solution.py:91
  220.2 2.4 collective-permute-start.5
  222.6 4.6 %collective-permute-done.5 = f32[2,1024]{1,0:T(2,128)S(1)} collective-permute-done((f32[2,1024]{1,0:T(2,128)S(1)}, f32[2,1024]{1,0:T(2,128)S(1)}, u32[]{:S(2)}, u32[]{:S(2)}) %collective-permute-start.5) | collective-permute-done | bytes 8224 | tf_op jit(solution)/shard_map/ppermute | solution.py:91
  227.2 5.0 %collective-permute-start.6 = (f32[2,1024]{1,0:T(2,128)S(1)}, f32[2,1024]{1,0:T(2,128)S(1)}, u32[]{:S(2)}, u32[]{:S(2)}) collective-permute-start(f32[2,1024]{1,0:T(2,128)S(1)} %pad_maximum_fusion.6), channel_id=1, source_target_pairs={{0,64},{16,80},{32,96},{48,112},{64,0},{80,16},{96,32},{112,48},{1... | collective-permute-start | bytes 24584 | tf_op jit(solution)/shard_map/ppermute | solution.py:91
  232.3 1.6 collective-permute-done.6
  233.9 7.3 %collective-permute-start.7 = (f32[2,1024]{1,0:T(2,128)S(1)}, f32[2,1024]{1,0:T(2,128)S(1)}, u32[]{:S(2)}, u32[]{:S(2)}) collective-permute-start(f32[2,1024]{1,0:T(2,128)S(1)} %pad_maximum_fusion.7), channel_id=1, source_target_pairs={{0,128},{16,144},{32,160},{48,176},{64,192},{80,208},{96,224},{112... | collective-permute-start | bytes 24584 | tf_op jit(solution)/shard_map/ppermute | solution.py:91
  241.2 1.6 collective-permute-done.7
  242.9 7.7 %collective-permute-start.8 = (f32[2,1024]{1,0:T(2,128)S(1)}, f32[2,1024]{1,0:T(2,128)S(1)}, u32[]{:S(2)}, u32[]{:S(2)}) collective-permute-start(f32[2,1024]{1,0:T(2,128)S(1)} %pad_maximum_fusion.8), channel_id=1, source_target_pairs={{0,256},{16,272},{32,288},{48,304},{64,320},{80,336},{96,352},{112... | collective-permute-start | bytes 24584 | tf_op jit(solution)/shard_map/ppermute | solution.py:100
  250.6 4.0 %collective-permute-start.9 = (f32[2,1024]{1,0:T(2,128)S(1)}, f32[2,1024]{1,0:T(2,128)S(1)}, u32[]{:S(2)}, u32[]{:S(2)}) collective-permute-start(f32[2,1024]{1,0:T(2,128)S(1)} %pad_maximum_fusion.8), channel_id=1, source_target_pairs={{0,512},{16,528},{32,544},{48,560},{64,576},{80,592},{96,608},{112... | collective-permute-start | bytes 24584 | tf_op jit(solution)/shard_map/ppermute | solution.py:101
  254.7 5.3 %collective-permute-done.9 = f32[2,1024]{1,0:T(2,128)S(1)} collective-permute-done((f32[2,1024]{1,0:T(2,128)S(1)}, f32[2,1024]{1,0:T(2,128)S(1)}, u32[]{:S(2)}, u32[]{:S(2)}) %collective-permute-start.9) | collective-permute-done | bytes 8224 | tf_op jit(solution)/shard_map/ppermute | solution.py:101
  260.4 0.8 fusion.18
  (58 shorter events, 2.3 us)
Async XLA Ops:
  7.2 180.9 %copy-start = (bf16[256,1024]{1,0:T(8,128)(2,1)S(1)}, bf16[256,1024]{1,0:T(8,128)(2,1)}, u32[]{:S(2)}) copy-start(bf16[256,1024]{1,0:T(8,128)(2,1)} %param.16) | copy-start | bytes 1572868
  7.2 5.2 %copy-start.4 = (s32[1,4096,16]{1,2,0:T(8,128)S(1)}, s32[1,4096,16]{1,2,0:T(8,128)}, u32[]{:S(2)}) copy-start(s32[1,4096,16]{1,2,0:T(8,128)} %param.12) | copy-start | bytes 786436
  7.2 5.4 %copy-start.5 = (s32[1,32,16]{1,2,0:T(8,128)S(1)}, s32[1,32,16]{1,2,0:T(8,128)}, u32[]{:S(2)}) copy-start(s32[1,32,16]{1,2,0:T(8,128)} %param.13) | copy-start | bytes 6148
  7.2 5.6 %copy-start.9 = (s32[16]{0:T(128)S(1)}, s32[16]{0:T(128)}, u32[]{:S(2)}) copy-start(s32[16]{0:T(128)} %param.15) | copy-start | bytes 196
  7.2 60.4 %all-gather.3.cloned.1.call-start = ((), (), s32[]{:S(2)}) async-start(), calls=%async_computation.1 | async-start | bytes 3342336 | tf_op jit(solution)/shard_map/all_gather | solution.py:168
  13.7 58.6 %copy-start.2 = (s32[1,32]{1,0:T(1,128)S(1)}, s32[1,32]{1,0:T(1,128)}, u32[]{:S(2)}) copy-start(s32[1,32]{1,0:T(1,128)} %param.14) | copy-start | bytes 388
  72.3 1.9 copy-start.1
  188.0 66.7 %copy-start.8 = (bf16[1024]{0:T(1024)(128)(2,1)S(1)}, bf16[1024]{0:T(1024)(128)(2,1)}, u32[]{:S(2)}) copy-start(bf16[1024]{0:T(1024)(128)(2,1)} %param.19) | copy-start | bytes 6148
  188.0 72.1 %copy-start.6 = (f32[1024]{0:T(1024)S(1)}, f32[1024]{0:T(1024)}, u32[]{:S(2)}) copy-start(f32[1024]{0:T(1024)} %param.18) | copy-start | bytes 12292
  188.0 72.1 %copy-start.7 = (f32[1024]{0:T(1024)S(1)}, f32[1024]{0:T(1024)}, u32[]{:S(2)}) copy-start(f32[1024]{0:T(1024)} %param.17) | copy-start | bytes 12292
  188.6 4.4 %collective-permute-start = (f32[2,1024]{1,0:T(2,128)S(1)}, f32[2,1024]{1,0:T(2,128)S(1)}, u32[]{:S(2)}, u32[]{:S(2)}) collective-permute-start(f32[2,1024]{1,0:T(2,128)S(1)} %pad_maximum_fusion), channel_id=1, source_target_pairs={{0,1},{1,0},{2,3},{3,2},{4,5},{5,4},{6,7},{7,6},{8,9},{9,8},{10,11... | collective-permute-start | bytes 24584 | tf_op jit(solution)/shard_map/ppermute | solution.py:91
  193.0 5.5 %collective-permute-start.1 = (f32[2,1024]{1,0:T(2,128)S(1)}, f32[2,1024]{1,0:T(2,128)S(1)}, u32[]{:S(2)}, u32[]{:S(2)}) collective-permute-start(f32[2,1024]{1,0:T(2,128)S(1)} %pad_maximum_fusion.1), channel_id=1, source_target_pairs={{0,2},{1,3},{2,0},{3,1},{4,6},{5,7},{6,4},{7,5},{8,10},{9,11},{10,... | collective-permute-start | bytes 24584 | tf_op jit(solution)/shard_map/ppermute | solution.py:91
  198.6 6.4 %collective-permute-start.2 = (f32[2,1024]{1,0:T(2,128)S(1)}, f32[2,1024]{1,0:T(2,128)S(1)}, u32[]{:S(2)}, u32[]{:S(2)}) collective-permute-start(f32[2,1024]{1,0:T(2,128)S(1)} %pad_maximum_fusion.2), channel_id=1, source_target_pairs={{0,4},{1,5},{2,6},{3,7},{4,0},{5,1},{6,2},{7,3},{8,12},{9,13},{10,... | collective-permute-start | bytes 24584 | tf_op jit(solution)/shard_map/ppermute | solution.py:91
  205.1 9.5 %collective-permute-start.3 = (f32[2,1024]{1,0:T(2,128)S(1)}, f32[2,1024]{1,0:T(2,128)S(1)}, u32[]{:S(2)}, u32[]{:S(2)}) collective-permute-start(f32[2,1024]{1,0:T(2,128)S(1)} %pad_maximum_fusion.3), channel_id=1, source_target_pairs={{0,8},{1,9},{2,10},{3,11},{4,12},{5,13},{6,14},{7,15},{8,0},{9,1},... | collective-permute-start | bytes 24584 | tf_op jit(solution)/shard_map/ppermute | solution.py:91
  214.6 5.5 %collective-permute-start.4 = (f32[2,1024]{1,0:T(2,128)S(1)}, f32[2,1024]{1,0:T(2,128)S(1)}, u32[]{:S(2)}, u32[]{:S(2)}) collective-permute-start(f32[2,1024]{1,0:T(2,128)S(1)} %pad_maximum_fusion.4), channel_id=1, source_target_pairs={{0,16},{16,0},{32,48},{48,32},{64,80},{80,64},{96,112},{112,96},{1... | collective-permute-start | bytes 24584 | tf_op jit(solution)/shard_map/ppermute | solution.py:91
  220.2 7.0 %collective-permute-start.5 = (f32[2,1024]{1,0:T(2,128)S(1)}, f32[2,1024]{1,0:T(2,128)S(1)}, u32[]{:S(2)}, u32[]{:S(2)}) collective-permute-start(f32[2,1024]{1,0:T(2,128)S(1)} %pad_maximum_fusion.5), channel_id=1, source_target_pairs={{0,32},{16,48},{32,0},{48,16},{64,96},{80,112},{96,64},{112,80},{1... | collective-permute-start | bytes 24584 | tf_op jit(solution)/shard_map/ppermute | solution.py:91
  227.2 6.6 %collective-permute-start.6 = (f32[2,1024]{1,0:T(2,128)S(1)}, f32[2,1024]{1,0:T(2,128)S(1)}, u32[]{:S(2)}, u32[]{:S(2)}) collective-permute-start(f32[2,1024]{1,0:T(2,128)S(1)} %pad_maximum_fusion.6), channel_id=1, source_target_pairs={{0,64},{16,80},{32,96},{48,112},{64,0},{80,16},{96,32},{112,48},{1... | collective-permute-start | bytes 24584 | tf_op jit(solution)/shard_map/ppermute | solution.py:91
  233.9 8.9 %collective-permute-start.7 = (f32[2,1024]{1,0:T(2,128)S(1)}, f32[2,1024]{1,0:T(2,128)S(1)}, u32[]{:S(2)}, u32[]{:S(2)}) collective-permute-start(f32[2,1024]{1,0:T(2,128)S(1)} %pad_maximum_fusion.7), channel_id=1, source_target_pairs={{0,128},{16,144},{32,160},{48,176},{64,192},{80,208},{96,224},{112... | collective-permute-start | bytes 24584 | tf_op jit(solution)/shard_map/ppermute | solution.py:91
  242.9 11.9 %collective-permute-start.8 = (f32[2,1024]{1,0:T(2,128)S(1)}, f32[2,1024]{1,0:T(2,128)S(1)}, u32[]{:S(2)}, u32[]{:S(2)}) collective-permute-start(f32[2,1024]{1,0:T(2,128)S(1)} %pad_maximum_fusion.8), channel_id=1, source_target_pairs={{0,256},{16,272},{32,288},{48,304},{64,320},{80,336},{96,352},{112... | collective-permute-start | bytes 24584 | tf_op jit(solution)/shard_map/ppermute | solution.py:100
  250.6 9.5 %collective-permute-start.9 = (f32[2,1024]{1,0:T(2,128)S(1)}, f32[2,1024]{1,0:T(2,128)S(1)}, u32[]{:S(2)}, u32[]{:S(2)}) collective-permute-start(f32[2,1024]{1,0:T(2,128)S(1)} %pad_maximum_fusion.8), channel_id=1, source_target_pairs={{0,512},{16,528},{32,544},{48,560},{64,576},{80,592},{96,608},{112... | collective-permute-start | bytes 24584 | tf_op jit(solution)/shard_map/ppermute | solution.py:101
  260.4 0.8 copy-start.3
Sparse Core Ops, SparseCore 0:
  11.3 56.3 all-gather.2

commit v4 on v3

--- a/solution.py
+++ b/solution.py
@@ -11,7 +11,7 @@
 norm_eps = 1e-05
 
 
-def pool_kernel(order_ref, ids_ref, counts_ref, slots_ref, hot_ref, own_ref, out_ref, hits_ref, cols_ref):
+def pool_kernel(order_ref, ids_ref, counts_ref, slots_ref, hot_ref, own_ref, out_ref, hits_ref, cols_ref, rows_ref):
     step = pl.program_id(0)
     block = order_ref[step]
     list_len = slots_ref.shape[1]
@@ -26,11 +26,15 @@
     def _():
         cols_ref[...] = jnp.zeros(cols_ref.shape, cols_ref.dtype)
 
+    low = slots % 128
+    high = slots // 128
+    for entry in range(list_len):
+        rows_ref[entry] = (low[entry : entry + 1, :] == row_iota).astype(jnp.float32)
+
     def place(k, carry):
-        shifted = slots - k * 128
         hits = jnp.zeros((128, 128), jnp.float32)
         for entry in range(list_len):
-            hits = hits + (shifted[entry : entry + 1, :] == row_iota).astype(jnp.float32)
+            hits = hits + jnp.where(high[entry : entry + 1, :] == k, rows_ref[entry], 0.0)
         start = pl.multiple_of(k * 128, 128)
         hits_ref[pl.ds(start, 128), :] = hits.astype(hits_ref.dtype)
         name = jnp.clip(ids_ref[block * list_len + k], 0, hot_count + own_count - 1)
@@ -75,6 +79,7 @@
         scratch_shapes=[
             pltpu.VMEM((bag_len * 128, 128), jnp.bfloat16),
             pltpu.VMEM((width, bag_len * 128), jnp.bfloat16),
+            pltpu.VMEM((bag_len, 128, 128), jnp.float32),
         ],
     )
     return pl.pallas_call(

time: 269 us -> 262 us (0.974)
  blocking collectives: 73.9 us -> 68.6 us
  starting transfers between devices: 39.8 us -> 36.8 us
    all_to_all x1, blocking collectives: 73.9 us -> 68.6 us  [shards(): lax.all_to_all(pooled, 'cache', split_axis=1, concat_axis=0, tiled=True)]
where the time goes in v4:
time: 262 us; the launch traced here: 261 us
  waiting for transfers between devices  87.1 us (33%)
  blocking collectives  68.6 us (26%)
  Pallas kernels  37 us (14%)
  starting transfers between devices  36.8 us (14%)
  between operations  14.5 us (6%)
  local copies, waits for them, and re-layouts  11.6 us (4%)
  other arithmetic  2.97 us (1%)
    all_to_all x1, blocking collectives, shards(): lax.all_to_all(pooled, 'cache', split_axis=1, concat_axis=0, tiled=True)  68.6 us
    all_gather x1, waiting for transfers between devices, shards(): gathered = lax.all_gather(hot_rows.T, 'cache', axis=0)  54 us
    pallas_call x1, Pallas kernels, pool(): pl.pallas_call(pool_kernel, grid_spec=grid_spec, out_shape=jax.ShapeDtype...  37 us
    ppermute x8, starting transfers between devices, merge_pair(): other = lax.ppermute(stats, axis, [(i, i ^ bit) for i in range(size)])  25.9 us
    ppermute x8, waiting for transfers between devices, merge_pair(): other = lax.ppermute(stats, axis, [(i, i ^ bit) for i in range(size)])  25.6 us
    ppermute x1, starting transfers between devices, merge_three(): lax.ppermute(stats, axis, [(i, (i + stride) % size) for i in range(size)])  8.98 us
    ppermute x1, waiting for transfers between devices, merge_three(): lax.ppermute(stats, axis, [(i, (i + 2 * stride) % size) for i in range(si...  7.51 us
  transfers between devices with their start and end apart: 11, of which 10 were waited for; matrix products, arithmetic and copies ran while one was open for 1% of the time, Pallas kernels for 0%

profile of v4, /device:TPU:6, one launch (start us, length us, event | category | flops | bytes accessed | tf_op | source)
XLA Modules:
  0.0 261.0 jit_solution(6326675907588198106)
XLA Ops:
  7.3 0.7 compare_select_fusion
  8.7 1.6 gather_fusion.1
  10.3 0.8 bitcast_select_fusion
  11.1 1.2 copy.38
  13.0 0.7 gather_fusion
  13.7 54.0 %all-gather.3.cloned.1.call-done = bf16[4096,384]{0,1:T(8,128)(2,1)} async-done(((bf16[256,384]{0,1:T(8,128)(2,1)}), bf16[4096,384]{0,1:T(8,128)(2,1)}) %all-gather.3.cloned.1.call-update) | async-done | bytes 3145744 | tf_op jit(solution)/shard_map/all_gather | solution.py:173
  67.6 4.7 %copy.37 = bf16[4096,384]{1,0:T(8,128)(2,1)} copy(bf16[4096,384]{0,1:T(8,128)(2,1)} %all-gather.3.cloned.1.call-done) | data formatting | bytes 6291456 | tf_op jit(solution)/shard_map/all_gather | solution.py:173
  72.3 1.9 copy-done.1
  74.2 37.0 %shard_map.113 = bf16[4096,256]{1,0:T(8,128)(2,1)S(1)} custom-call(s32[32]{0:T(128)S(1)} %fusion.12.order_ref, s32[512]{0:T(512)S(1)} %reshape.146.ids_ref, s32[32]{0:T(128)S(1)} %bitcast.39, s32[32,16,128]{2,1,0:T(8,128)S(1)} %bitcast.38, bf16[16,256,384]{2,1,0:T(8,128)(2,1)S(1)} %bitcast.35, bf16[256,1024]{1,0:T(8,128)(2,1)S(1)} %bitcast.37), custom_call_target="tpu_custom_call" | custom-call | tf_op jit(solution)/shard_map/pallas_call | solution.py:85
  111.2 68.6 %all_to_all.4 = bf16[1,16,256,256]{3,2,0,1:T(8,128)(2,1)S(1)} all-to-all(bf16[1,16,256,256]{3,2,0,1:T(8,128)(2,1)S(1)} %bitcast.36), channel_id=1, replica_groups=mesh['shard'=48,'cache'=16] {'cache'}, dimensions={1} | all-to-all | bytes 4194304 | tf_op jit(solution)/shard_map/all_to_all | solution.py:176
  179.8 1.3 fusion
  181.1 1.0 copy.41
  182.7 3.6 %collective-permute-start = (f32[2,1024]{1,0:T(2,128)S(1)}, f32[2,1024]{1,0:T(2,128)S(1)}, u32[]{:S(2)}, u32[]{:S(2)}) collective-permute-start(f32[2,1024]{1,0:T(2,128)S(1)} %pad_maximum_fusion), channel_id=1, source_target_pairs={{0,1},{1,0},{2,3},{3,2},{4,5},{5,4},{6,7},{7,6},{8,9},{9,8},{10,11... | collective-permute-start | bytes 24584 | tf_op jit(solution)/shard_map/ppermute | solution.py:96
  186.3 0.8 collective-permute-done
  187.1 1.9 collective-permute-start.1
  189.0 3.6 %collective-permute-done.1 = f32[2,1024]{1,0:T(2,128)S(1)} collective-permute-done((f32[2,1024]{1,0:T(2,128)S(1)}, f32[2,1024]{1,0:T(2,128)S(1)}, u32[]{:S(2)}, u32[]{:S(2)}) %collective-permute-start.1) | collective-permute-done | bytes 8224 | tf_op jit(solution)/shard_map/ppermute | solution.py:96
  192.7 2.4 collective-permute-start.2
  195.1 4.1 %collective-permute-done.2 = f32[2,1024]{1,0:T(2,128)S(1)} collective-permute-done((f32[2,1024]{1,0:T(2,128)S(1)}, f32[2,1024]{1,0:T(2,128)S(1)}, u32[]{:S(2)}, u32[]{:S(2)}) %collective-permute-start.2) | collective-permute-done | bytes 8224 | tf_op jit(solution)/shard_map/ppermute | solution.py:96
  199.2 3.4 %collective-permute-start.3 = (f32[2,1024]{1,0:T(2,128)S(1)}, f32[2,1024]{1,0:T(2,128)S(1)}, u32[]{:S(2)}, u32[]{:S(2)}) collective-permute-start(f32[2,1024]{1,0:T(2,128)S(1)} %pad_maximum_fusion.3), channel_id=1, source_target_pairs={{0,8},{1,9},{2,10},{3,11},{4,12},{5,13},{6,14},{7,15},{8,0},{9,1},... | collective-permute-start | bytes 24584 | tf_op jit(solution)/shard_map/ppermute | solution.py:96
  202.6 6.0 %collective-permute-done.3 = f32[2,1024]{1,0:T(2,128)S(1)} collective-permute-done((f32[2,1024]{1,0:T(2,128)S(1)}, f32[2,1024]{1,0:T(2,128)S(1)}, u32[]{:S(2)}, u32[]{:S(2)}) %collective-permute-start.3) | collective-permute-done | bytes 8224 | tf_op jit(solution)/shard_map/ppermute | solution.py:96
  208.7 1.9 collective-permute-start.4
  210.6 3.6 %collective-permute-done.4 = f32[2,1024]{1,0:T(2,128)S(1)} collective-permute-done((f32[2,1024]{1,0:T(2,128)S(1)}, f32[2,1024]{1,0:T(2,128)S(1)}, u32[]{:S(2)}, u32[]{:S(2)}) %collective-permute-start.4) | collective-permute-done | bytes 8224 | tf_op jit(solution)/shard_map/ppermute | solution.py:96
  214.3 3.1 %collective-permute-start.5 = (f32[2,1024]{1,0:T(2,128)S(1)}, f32[2,1024]{1,0:T(2,128)S(1)}, u32[]{:S(2)}, u32[]{:S(2)}) collective-permute-start(f32[2,1024]{1,0:T(2,128)S(1)} %pad_maximum_fusion.5), channel_id=1, source_target_pairs={{0,32},{16,48},{32,0},{48,16},{64,96},{80,112},{96,64},{112,80},{1... | collective-permute-start | bytes 24584 | tf_op jit(solution)/shard_map/ppermute | solution.py:96
  217.3 4.0 %collective-permute-done.5 = f32[2,1024]{1,0:T(2,128)S(1)} collective-permute-done((f32[2,1024]{1,0:T(2,128)S(1)}, f32[2,1024]{1,0:T(2,128)S(1)}, u32[]{:S(2)}, u32[]{:S(2)}) %collective-permute-start.5) | collective-permute-done | bytes 8224 | tf_op jit(solution)/shard_map/ppermute | solution.py:96
  221.3 3.6 %collective-permute-start.6 = (f32[2,1024]{1,0:T(2,128)S(1)}, f32[2,1024]{1,0:T(2,128)S(1)}, u32[]{:S(2)}, u32[]{:S(2)}) collective-permute-start(f32[2,1024]{1,0:T(2,128)S(1)} %pad_maximum_fusion.6), channel_id=1, source_target_pairs={{0,64},{16,80},{32,96},{48,112},{64,0},{80,16},{96,32},{112,48},{1... | collective-permute-start | bytes 24584 | tf_op jit(solution)/shard_map/ppermute | solution.py:96
  225.0 1.9 collective-permute-done.6
  226.9 5.9 %collective-permute-start.7 = (f32[2,1024]{1,0:T(2,128)S(1)}, f32[2,1024]{1,0:T(2,128)S(1)}, u32[]{:S(2)}, u32[]{:S(2)}) collective-permute-start(f32[2,1024]{1,0:T(2,128)S(1)} %pad_maximum_fusion.7), channel_id=1, source_target_pairs={{0,128},{16,144},{32,160},{48,176},{64,192},{80,208},{96,224},{112... | collective-permute-start | bytes 24584 | tf_op jit(solution)/shard_map/ppermute | solution.py:96
  232.9 1.6 collective-permute-done.7
  234.5 9.0 %collective-permute-start.8 = (f32[2,1024]{1,0:T(2,128)S(1)}, f32[2,1024]{1,0:T(2,128)S(1)}, u32[]{:S(2)}, u32[]{:S(2)}) collective-permute-start(f32[2,1024]{1,0:T(2,128)S(1)} %pad_maximum_fusion.8), channel_id=1, source_target_pairs={{0,256},{16,272},{32,288},{48,304},{64,320},{80,336},{96,352},{112... | collective-permute-start | bytes 24584 | tf_op jit(solution)/shard_map/ppermute | solution.py:105
  243.5 1.9 collective-permute-start.9
  245.5 7.5 %collective-permute-done.9 = f32[2,1024]{1,0:T(2,128)S(1)} collective-permute-done((f32[2,1024]{1,0:T(2,128)S(1)}, f32[2,1024]{1,0:T(2,128)S(1)}, u32[]{:S(2)}, u32[]{:S(2)}) %collective-permute-start.9) | collective-permute-done | bytes 8224 | tf_op jit(solution)/shard_map/ppermute | solution.py:106
  253.3 0.8 fusion.18
  (58 shorter events, 2.3 us)
Async XLA Ops:
  7.2 175.0 %copy-start = (bf16[256,1024]{1,0:T(8,128)(2,1)S(1)}, bf16[256,1024]{1,0:T(8,128)(2,1)}, u32[]{:S(2)}) copy-start(bf16[256,1024]{1,0:T(8,128)(2,1)} %param.16) | copy-start | bytes 1572868
  7.2 5.2 %copy-start.4 = (s32[1,4096,16]{1,2,0:T(8,128)S(1)}, s32[1,4096,16]{1,2,0:T(8,128)}, u32[]{:S(2)}) copy-start(s32[1,4096,16]{1,2,0:T(8,128)} %param.12) | copy-start | bytes 786436
  7.2 5.4 %copy-start.5 = (s32[1,32,16]{1,2,0:T(8,128)S(1)}, s32[1,32,16]{1,2,0:T(8,128)}, u32[]{:S(2)}) copy-start(s32[1,32,16]{1,2,0:T(8,128)} %param.13) | copy-start | bytes 6148
  7.2 5.6 %copy-start.9 = (s32[16]{0:T(128)S(1)}, s32[16]{0:T(128)}, u32[]{:S(2)}) copy-start(s32[16]{0:T(128)} %param.15) | copy-start | bytes 196
  7.2 60.4 %all-gather.3.cloned.1.call-start = ((), (), s32[]{:S(2)}) async-start(), calls=%async_computation.1 | async-start | bytes 3342336 | tf_op jit(solution)/shard_map/all_gather | solution.py:173
  13.7 58.6 %copy-start.2 = (s32[1,32]{1,0:T(1,128)S(1)}, s32[1,32]{1,0:T(1,128)}, u32[]{:S(2)}) copy-start(s32[1,32]{1,0:T(1,128)} %param.14) | copy-start | bytes 388
  72.3 1.9 copy-start.1
  182.1 63.4 %copy-start.8 = (bf16[1024]{0:T(1024)(128)(2,1)S(1)}, bf16[1024]{0:T(1024)(128)(2,1)}, u32[]{:S(2)}) copy-start(bf16[1024]{0:T(1024)(128)(2,1)} %param.19) | copy-start | bytes 6148
  182.1 71.0 %copy-start.6 = (f32[1024]{0:T(1024)S(1)}, f32[1024]{0:T(1024)}, u32[]{:S(2)}) copy-start(f32[1024]{0:T(1024)} %param.18) | copy-start | bytes 12292
  182.1 71.0 %copy-start.7 = (f32[1024]{0:T(1024)S(1)}, f32[1024]{0:T(1024)}, u32[]{:S(2)}) copy-start(f32[1024]{0:T(1024)} %param.17) | copy-start | bytes 12292
  182.7 4.4 %collective-permute-start = (f32[2,1024]{1,0:T(2,128)S(1)}, f32[2,1024]{1,0:T(2,128)S(1)}, u32[]{:S(2)}, u32[]{:S(2)}) collective-permute-start(f32[2,1024]{1,0:T(2,128)S(1)} %pad_maximum_fusion), channel_id=1, source_target_pairs={{0,1},{1,0},{2,3},{3,2},{4,5},{5,4},{6,7},{7,6},{8,9},{9,8},{10,11... | collective-permute-start | bytes 24584 | tf_op jit(solution)/shard_map/ppermute | solution.py:96
  187.1 5.5 %collective-permute-start.1 = (f32[2,1024]{1,0:T(2,128)S(1)}, f32[2,1024]{1,0:T(2,128)S(1)}, u32[]{:S(2)}, u32[]{:S(2)}) collective-permute-start(f32[2,1024]{1,0:T(2,128)S(1)} %pad_maximum_fusion.1), channel_id=1, source_target_pairs={{0,2},{1,3},{2,0},{3,1},{4,6},{5,7},{6,4},{7,5},{8,10},{9,11},{10,... | collective-permute-start | bytes 24584 | tf_op jit(solution)/shard_map/ppermute | solution.py:96
  192.7 6.4 %collective-permute-start.2 = (f32[2,1024]{1,0:T(2,128)S(1)}, f32[2,1024]{1,0:T(2,128)S(1)}, u32[]{:S(2)}, u32[]{:S(2)}) collective-permute-start(f32[2,1024]{1,0:T(2,128)S(1)} %pad_maximum_fusion.2), channel_id=1, source_target_pairs={{0,4},{1,5},{2,6},{3,7},{4,0},{5,1},{6,2},{7,3},{8,12},{9,13},{10,... | collective-permute-start | bytes 24584 | tf_op jit(solution)/shard_map/ppermute | solution.py:96
  199.2 9.5 %collective-permute-start.3 = (f32[2,1024]{1,0:T(2,128)S(1)}, f32[2,1024]{1,0:T(2,128)S(1)}, u32[]{:S(2)}, u32[]{:S(2)}) collective-permute-start(f32[2,1024]{1,0:T(2,128)S(1)} %pad_maximum_fusion.3), channel_id=1, source_target_pairs={{0,8},{1,9},{2,10},{3,11},{4,12},{5,13},{6,14},{7,15},{8,0},{9,1},... | collective-permute-start | bytes 24584 | tf_op jit(solution)/shard_map/ppermute | solution.py:96
  208.7 5.5 %collective-permute-start.4 = (f32[2,1024]{1,0:T(2,128)S(1)}, f32[2,1024]{1,0:T(2,128)S(1)}, u32[]{:S(2)}, u32[]{:S(2)}) collective-permute-start(f32[2,1024]{1,0:T(2,128)S(1)} %pad_maximum_fusion.4), channel_id=1, source_target_pairs={{0,16},{16,0},{32,48},{48,32},{64,80},{80,64},{96,112},{112,96},{1... | collective-permute-start | bytes 24584 | tf_op jit(solution)/shard_map/ppermute | solution.py:96
  214.3 7.0 %collective-permute-start.5 = (f32[2,1024]{1,0:T(2,128)S(1)}, f32[2,1024]{1,0:T(2,128)S(1)}, u32[]{:S(2)}, u32[]{:S(2)}) collective-permute-start(f32[2,1024]{1,0:T(2,128)S(1)} %pad_maximum_fusion.5), channel_id=1, source_target_pairs={{0,32},{16,48},{32,0},{48,16},{64,96},{80,112},{96,64},{112,80},{1... | collective-permute-start | bytes 24584 | tf_op jit(solution)/shard_map/ppermute | solution.py:96
  221.3 5.5 %collective-permute-start.6 = (f32[2,1024]{1,0:T(2,128)S(1)}, f32[2,1024]{1,0:T(2,128)S(1)}, u32[]{:S(2)}, u32[]{:S(2)}) collective-permute-start(f32[2,1024]{1,0:T(2,128)S(1)} %pad_maximum_fusion.6), channel_id=1, source_target_pairs={{0,64},{16,80},{32,96},{48,112},{64,0},{80,16},{96,32},{112,48},{1... | collective-permute-start | bytes 24584 | tf_op jit(solution)/shard_map/ppermute | solution.py:96
  226.9 7.6 %collective-permute-start.7 = (f32[2,1024]{1,0:T(2,128)S(1)}, f32[2,1024]{1,0:T(2,128)S(1)}, u32[]{:S(2)}, u32[]{:S(2)}) collective-permute-start(f32[2,1024]{1,0:T(2,128)S(1)} %pad_maximum_fusion.7), channel_id=1, source_target_pairs={{0,128},{16,144},{32,160},{48,176},{64,192},{80,208},{96,224},{112... | collective-permute-start | bytes 24584 | tf_op jit(solution)/shard_map/ppermute | solution.py:96
  234.5 11.0 %collective-permute-start.8 = (f32[2,1024]{1,0:T(2,128)S(1)}, f32[2,1024]{1,0:T(2,128)S(1)}, u32[]{:S(2)}, u32[]{:S(2)}) collective-permute-start(f32[2,1024]{1,0:T(2,128)S(1)} %pad_maximum_fusion.8), channel_id=1, source_target_pairs={{0,256},{16,272},{32,288},{48,304},{64,320},{80,336},{96,352},{112... | collective-permute-start | bytes 24584 | tf_op jit(solution)/shard_map/ppermute | solution.py:105
  243.5 9.5 %collective-permute-start.9 = (f32[2,1024]{1,0:T(2,128)S(1)}, f32[2,1024]{1,0:T(2,128)S(1)}, u32[]{:S(2)}, u32[]{:S(2)}) collective-permute-start(f32[2,1024]{1,0:T(2,128)S(1)} %pad_maximum_fusion.8), channel_id=1, source_target_pairs={{0,512},{16,528},{32,544},{48,560},{64,576},{80,592},{96,608},{112... | collective-permute-start | bytes 24584 | tf_op jit(solution)/shard_map/ppermute | solution.py:106
  253.3 0.8 copy-start.3
Sparse Core Ops, SparseCore 0:
  11.3 56.3 all-gather.2

commit v5 on v4

--- a/solution.py
+++ b/solution.py
@@ -155,7 +155,6 @@
     group_blocks = group_samp // 128
     blocks_dev = feat_dev * group_blocks
     list_len = block_ids.shape[2]
-    hot_rows = jnp.take(table.reshape(-1, 128, row_width), panel_ids, axis=0).reshape(-1, row_width)
     cache_ids = jnp.arange(caches, dtype=jnp.int32)
     owner_match = dense_owner[None, :] == cache_ids[:, None]
     inverse = jnp.sum(jnp.where(owner_match, cache_ids[None, :], 0), axis=1)
@@ -170,8 +169,10 @@
     slots_t = jnp.swapaxes(bag_slots.reshape(blocks_dev, 128, bag_len), 1, 2)
     ids = block_ids.reshape(blocks_dev * list_len).astype(jnp.int32)
     counts = bag_counts.reshape(blocks_dev).astype(jnp.int32)
-    gathered = lax.all_gather(hot_rows.T, "cache", axis=0)
-    pooled = pool(source_block, ids, counts, slots_t, gathered, table.T)
+    own_t = table.T
+    hot_t = jnp.take(own_t.reshape(row_width, -1, 128), panel_ids, axis=1).reshape(row_width, -1)
+    gathered = lax.all_gather(hot_t, "cache", axis=0)
+    pooled = pool(source_block, ids, counts, slots_t, gathered, own_t)
     pooled = pooled.reshape(feat_dev, caches, samp_dev, row_width)
     features = lax.all_to_all(pooled, "cache", split_axis=1, concat_axis=0, tiled=True)[:, 0]
     products = jnp.einsum("fne,gne->nfg", features, features, preferred_element_type=jnp.float32)

time: 262 us -> 253 us (0.966)
  waiting for transfers between devices: 87.1 us -> 80.5 us
  Pallas kernels: 37 us -> 31.8 us
  local copies, waits for them, and re-layouts: 11.6 us -> 6.98 us
  starting transfers between devices: 36.8 us -> 40.8 us
  blocking collectives: 68.6 us -> 72.1 us
    pallas_call x1, Pallas kernels: 37 us -> 31.8 us  [pool(): pl.pallas_call(pool_kernel, grid_spec=grid_spec, out_shape=jax.ShapeDtype...]
    all_gather x1 -> x0, local copies, waits for them, and re-layouts: 4.65 us -> none  [shards(): gathered = lax.all_gather(hot_rows.T, 'cache', axis=0)]
    ppermute x8, starting transfers between devices: 25.9 us -> 29.5 us  [merge_pair(): other = lax.ppermute(stats, axis, [(i, i ^ bit) for i in range(size)])]
    all_to_all x1, blocking collectives: 68.6 us -> 72.1 us  [shards(): lax.all_to_all(pooled, 'cache', split_axis=1, concat_axis=0, tiled=True)]
    all_gather x1, waiting for transfers between devices: 54 us -> 51.3 us  [shards(): gathered = lax.all_gather(hot_t, 'cache', axis=0)]
  transfers between devices with their start and end apart: 11 -> 11, of which waited for: 10 -> 10; matrix products, arithmetic and copies ran while one was open for 1% -> 0% of each run, Pallas kernels for 0% -> 0%
where the time goes in v5:
time: 253 us; the launch traced here: 251 us
  waiting for transfers between devices  80.5 us (32%)
  blocking collectives  72.1 us (28%)
  starting transfers between devices  40.8 us (16%)
  Pallas kernels  31.8 us (13%)
  between operations  14.5 us (6%)
  local copies, waits for them, and re-layouts  6.98 us (3%)
    all_to_all x1, blocking collectives, shards(): lax.all_to_all(pooled, 'cache', split_axis=1, concat_axis=0, tiled=True)  72.1 us
    all_gather x1, waiting for transfers between devices, shards(): gathered = lax.all_gather(hot_t, 'cache', axis=0)  51.3 us
    pallas_call x1, Pallas kernels, pool(): pl.pallas_call(pool_kernel, grid_spec=grid_spec, out_shape=jax.ShapeDtype...  31.8 us
    ppermute x8, starting transfers between devices, merge_pair(): other = lax.ppermute(stats, axis, [(i, i ^ bit) for i in range(size)])  29.5 us
    ppermute x8, waiting for transfers between devices, merge_pair(): other = lax.ppermute(stats, axis, [(i, i ^ bit) for i in range(size)])  23.4 us
    ppermute x1, starting transfers between devices, merge_three(): lax.ppermute(stats, axis, [(i, (i + stride) % size) for i in range(size)])  7.65 us
    ppermute x1, waiting for transfers between devices, merge_three(): lax.ppermute(stats, axis, [(i, (i + 2 * stride) % size) for i in range(si...  5.74 us
  transfers between devices with their start and end apart: 11, of which 10 were waited for; matrix products, arithmetic and copies ran while one was open for 0% of the time, Pallas kernels for 0%

profile of v5, /device:TPU:6, one launch (start us, length us, event | category | flops | bytes accessed | tf_op | source)
XLA Modules:
  0.0 251.4 jit_solution(11542623430587493656)
XLA Ops:
  7.2 0.7 compare_select_fusion
  8.0 0.7 compare_and_fusion
  8.6 1.2 copy.42
  10.0 0.6 gather_fusion.1
  11.0 0.8 copy.45
  12.4 0.7 gather_fusion
  13.1 51.3 %all-gather.2.cloned.1.call-done.hot_ref = bf16[16,256,384]{2,1,0:T(8,128)(2,1)} async-done(((bf16[1,256,384]{2,1,0:T(8,128)(2,1)}), bf16[16,256,384]{2,1,0:T(8,128)(2,1)}) %all-gather.2.cloned.1.call-update) | async-done | bytes 3145744 | tf_op jit(solution)/shard_map/all_gather | solution.py:174
  64.4 1.9 copy-done.1
  66.3 31.8 %shard_map.113 = bf16[4096,256]{1,0:T(8,128)(2,1)S(1)} custom-call(s32[32]{0:T(128)S(1)} %fusion.12.order_ref, s32[512]{0:T(512)S(1)} %reshape.172.ids_ref, s32[32]{0:T(128)S(1)} %bitcast.41, s32[32,16,128]{2,1,0:T(8,128)S(1)} %bitcast.40, bf16[16,256,384]{2,1,0:T(8,128)(2,1)S(1)} %copy-done.1, bf16[256,1024]{1,0:T(8,128)(2,1)S(1)} %bitcast.39), custom_call_target="tpu_custom_call" | custom-call | tf_op jit(solution)/shard_map/pallas_call | solution.py:85
  98.1 72.1 %all_to_all.4 = bf16[1,16,256,256]{3,2,0,1:T(8,128)(2,1)S(1)} all-to-all(bf16[1,16,256,256]{3,2,0,1:T(8,128)(2,1)S(1)} %bitcast.38), channel_id=1, replica_groups=mesh['shard'=48,'cache'=16] {'cache'}, dimensions={1} | all-to-all | bytes 4194304 | tf_op jit(solution)/shard_map/all_to_all | solution.py:177
  170.1 1.3 fusion
  171.4 1.0 copy.48
  173.0 3.6 %collective-permute-start = (f32[2,1024]{1,0:T(2,128)S(1)}, f32[2,1024]{1,0:T(2,128)S(1)}, u32[]{:S(2)}, u32[]{:S(2)}) collective-permute-start(f32[2,1024]{1,0:T(2,128)S(1)} %pad_maximum_fusion), channel_id=1, source_target_pairs={{0,1},{1,0},{2,3},{3,2},{4,5},{5,4},{6,7},{7,6},{8,9},{9,8},{10,11... | collective-permute-start | bytes 24584 | tf_op jit(solution)/shard_map/ppermute | solution.py:96
  176.6 0.8 collective-permute-done
  177.4 1.9 collective-permute-start.1
  179.3 3.6 %collective-permute-done.1 = f32[2,1024]{1,0:T(2,128)S(1)} collective-permute-done((f32[2,1024]{1,0:T(2,128)S(1)}, f32[2,1024]{1,0:T(2,128)S(1)}, u32[]{:S(2)}, u32[]{:S(2)}) %collective-permute-start.1) | collective-permute-done | bytes 8224 | tf_op jit(solution)/shard_map/ppermute | solution.py:96
  183.0 2.4 collective-permute-start.2
  185.4 4.1 %collective-permute-done.2 = f32[2,1024]{1,0:T(2,128)S(1)} collective-permute-done((f32[2,1024]{1,0:T(2,128)S(1)}, f32[2,1024]{1,0:T(2,128)S(1)}, u32[]{:S(2)}, u32[]{:S(2)}) %collective-permute-start.2) | collective-permute-done | bytes 8224 | tf_op jit(solution)/shard_map/ppermute | solution.py:96
  189.5 3.4 %collective-permute-start.3 = (f32[2,1024]{1,0:T(2,128)S(1)}, f32[2,1024]{1,0:T(2,128)S(1)}, u32[]{:S(2)}, u32[]{:S(2)}) collective-permute-start(f32[2,1024]{1,0:T(2,128)S(1)} %pad_maximum_fusion.3), channel_id=1, source_target_pairs={{0,8},{1,9},{2,10},{3,11},{4,12},{5,13},{6,14},{7,15},{8,0},{9,1},... | collective-permute-start | bytes 24584 | tf_op jit(solution)/shard_map/ppermute | solution.py:96
  192.9 6.0 %collective-permute-done.3 = f32[2,1024]{1,0:T(2,128)S(1)} collective-permute-done((f32[2,1024]{1,0:T(2,128)S(1)}, f32[2,1024]{1,0:T(2,128)S(1)}, u32[]{:S(2)}, u32[]{:S(2)}) %collective-permute-start.3) | collective-permute-done | bytes 8224 | tf_op jit(solution)/shard_map/ppermute | solution.py:96
  199.0 1.9 collective-permute-start.4
  200.9 3.6 %collective-permute-done.4 = f32[2,1024]{1,0:T(2,128)S(1)} collective-permute-done((f32[2,1024]{1,0:T(2,128)S(1)}, f32[2,1024]{1,0:T(2,128)S(1)}, u32[]{:S(2)}, u32[]{:S(2)}) %collective-permute-start.4) | collective-permute-done | bytes 8224 | tf_op jit(solution)/shard_map/ppermute | solution.py:96
  204.6 5.7 %collective-permute-start.5 = (f32[2,1024]{1,0:T(2,128)S(1)}, f32[2,1024]{1,0:T(2,128)S(1)}, u32[]{:S(2)}, u32[]{:S(2)}) collective-permute-start(f32[2,1024]{1,0:T(2,128)S(1)} %pad_maximum_fusion.5), channel_id=1, source_target_pairs={{0,32},{16,48},{32,0},{48,16},{64,96},{80,112},{96,64},{112,80},{1... | collective-permute-start | bytes 24584 | tf_op jit(solution)/shard_map/ppermute | solution.py:96
  210.3 1.6 collective-permute-done.5
  211.9 6.2 %collective-permute-start.6 = (f32[2,1024]{1,0:T(2,128)S(1)}, f32[2,1024]{1,0:T(2,128)S(1)}, u32[]{:S(2)}, u32[]{:S(2)}) collective-permute-start(f32[2,1024]{1,0:T(2,128)S(1)} %pad_maximum_fusion.6), channel_id=1, source_target_pairs={{0,64},{16,80},{32,96},{48,112},{64,0},{80,16},{96,32},{112,48},{1... | collective-permute-start | bytes 24584 | tf_op jit(solution)/shard_map/ppermute | solution.py:96
  218.1 1.6 collective-permute-done.6
  219.8 4.4 %collective-permute-start.7 = (f32[2,1024]{1,0:T(2,128)S(1)}, f32[2,1024]{1,0:T(2,128)S(1)}, u32[]{:S(2)}, u32[]{:S(2)}) collective-permute-start(f32[2,1024]{1,0:T(2,128)S(1)} %pad_maximum_fusion.7), channel_id=1, source_target_pairs={{0,128},{16,144},{32,160},{48,176},{64,192},{80,208},{96,224},{112... | collective-permute-start | bytes 24584 | tf_op jit(solution)/shard_map/ppermute | solution.py:96
  224.2 2.1 collective-permute-done.7
  226.3 7.7 %collective-permute-start.8 = (f32[2,1024]{1,0:T(2,128)S(1)}, f32[2,1024]{1,0:T(2,128)S(1)}, u32[]{:S(2)}, u32[]{:S(2)}) collective-permute-start(f32[2,1024]{1,0:T(2,128)S(1)} %pad_maximum_fusion.8), channel_id=1, source_target_pairs={{0,256},{16,272},{32,288},{48,304},{64,320},{80,336},{96,352},{112... | collective-permute-start | bytes 24584 | tf_op jit(solution)/shard_map/ppermute | solution.py:105
  233.9 3.6 %collective-permute-start.9 = (f32[2,1024]{1,0:T(2,128)S(1)}, f32[2,1024]{1,0:T(2,128)S(1)}, u32[]{:S(2)}, u32[]{:S(2)}) collective-permute-start(f32[2,1024]{1,0:T(2,128)S(1)} %pad_maximum_fusion.8), channel_id=1, source_target_pairs={{0,512},{16,528},{32,544},{48,560},{64,576},{80,592},{96,608},{112... | collective-permute-start | bytes 24584 | tf_op jit(solution)/shard_map/ppermute | solution.py:106
  237.6 5.7 %collective-permute-done.9 = f32[2,1024]{1,0:T(2,128)S(1)} collective-permute-done((f32[2,1024]{1,0:T(2,128)S(1)}, f32[2,1024]{1,0:T(2,128)S(1)}, u32[]{:S(2)}, u32[]{:S(2)}) %collective-permute-start.9) | collective-permute-done | bytes 8224 | tf_op jit(solution)/shard_map/ppermute | solution.py:106
  243.7 0.8 fusion.18
  (60 shorter events, 2.0 us)
Async XLA Ops:
  7.2 165.3 %copy-start = (bf16[256,1024]{1,0:T(8,128)(2,1)S(1)}, bf16[256,1024]{1,0:T(8,128)(2,1)}, u32[]{:S(2)}) copy-start(bf16[256,1024]{1,0:T(8,128)(2,1)} %param.16) | copy-start | bytes 1572868
  7.2 4.6 %copy-start.4 = (s32[1,4096,16]{1,2,0:T(8,128)S(1)}, s32[1,4096,16]{1,2,0:T(8,128)}, u32[]{:S(2)}) copy-start(s32[1,4096,16]{1,2,0:T(8,128)} %param.12) | copy-start | bytes 786436
  7.2 57.2 %all-gather.2.cloned.1.call-start = ((), (), s32[]{:S(2)}) async-start(), calls=%async_computation.1 | async-start | bytes 3342336 | tf_op jit(solution)/shard_map/all_gather | solution.py:174
  9.9 2.2 copy-start.5
  9.9 2.4 copy-start.9
  9.9 54.5 %copy-start.2 = (s32[1,32]{1,0:T(1,128)S(1)}, s32[1,32]{1,0:T(1,128)}, u32[]{:S(2)}) copy-start(s32[1,32]{1,0:T(1,128)} %param.14) | copy-start | bytes 388
  64.4 1.9 copy-start.1
  172.4 65.2 %copy-start.8 = (bf16[1024]{0:T(1024)(128)(2,1)S(1)}, bf16[1024]{0:T(1024)(128)(2,1)}, u32[]{:S(2)}) copy-start(bf16[1024]{0:T(1024)(128)(2,1)} %param.19) | copy-start | bytes 6148
  172.4 71.0 %copy-start.6 = (f32[1024]{0:T(1024)S(1)}, f32[1024]{0:T(1024)}, u32[]{:S(2)}) copy-start(f32[1024]{0:T(1024)} %param.18) | copy-start | bytes 12292
  172.4 71.0 %copy-start.7 = (f32[1024]{0:T(1024)S(1)}, f32[1024]{0:T(1024)}, u32[]{:S(2)}) copy-start(f32[1024]{0:T(1024)} %param.17) | copy-start | bytes 12292
  173.0 4.4 %collective-permute-start = (f32[2,1024]{1,0:T(2,128)S(1)}, f32[2,1024]{1,0:T(2,128)S(1)}, u32[]{:S(2)}, u32[]{:S(2)}) collective-permute-start(f32[2,1024]{1,0:T(2,128)S(1)} %pad_maximum_fusion), channel_id=1, source_target_pairs={{0,1},{1,0},{2,3},{3,2},{4,5},{5,4},{6,7},{7,6},{8,9},{9,8},{10,11... | collective-permute-start | bytes 24584 | tf_op jit(solution)/shard_map/ppermute | solution.py:96
  177.4 5.5 %collective-permute-start.1 = (f32[2,1024]{1,0:T(2,128)S(1)}, f32[2,1024]{1,0:T(2,128)S(1)}, u32[]{:S(2)}, u32[]{:S(2)}) collective-permute-start(f32[2,1024]{1,0:T(2,128)S(1)} %pad_maximum_fusion.1), channel_id=1, source_target_pairs={{0,2},{1,3},{2,0},{3,1},{4,6},{5,7},{6,4},{7,5},{8,10},{9,11},{10,... | collective-permute-start | bytes 24584 | tf_op jit(solution)/shard_map/ppermute | solution.py:96
  183.0 6.4 %collective-permute-start.2 = (f32[2,1024]{1,0:T(2,128)S(1)}, f32[2,1024]{1,0:T(2,128)S(1)}, u32[]{:S(2)}, u32[]{:S(2)}) collective-permute-start(f32[2,1024]{1,0:T(2,128)S(1)} %pad_maximum_fusion.2), channel_id=1, source_target_pairs={{0,4},{1,5},{2,6},{3,7},{4,0},{5,1},{6,2},{7,3},{8,12},{9,13},{10,... | collective-permute-start | bytes 24584 | tf_op jit(solution)/shard_map/ppermute | solution.py:96
  189.5 9.5 %collective-permute-start.3 = (f32[2,1024]{1,0:T(2,128)S(1)}, f32[2,1024]{1,0:T(2,128)S(1)}, u32[]{:S(2)}, u32[]{:S(2)}) collective-permute-start(f32[2,1024]{1,0:T(2,128)S(1)} %pad_maximum_fusion.3), channel_id=1, source_target_pairs={{0,8},{1,9},{2,10},{3,11},{4,12},{5,13},{6,14},{7,15},{8,0},{9,1},... | collective-permute-start | bytes 24584 | tf_op jit(solution)/shard_map/ppermute | solution.py:96
  199.0 5.5 %collective-permute-start.4 = (f32[2,1024]{1,0:T(2,128)S(1)}, f32[2,1024]{1,0:T(2,128)S(1)}, u32[]{:S(2)}, u32[]{:S(2)}) collective-permute-start(f32[2,1024]{1,0:T(2,128)S(1)} %pad_maximum_fusion.4), channel_id=1, source_target_pairs={{0,16},{16,0},{32,48},{48,32},{64,80},{80,64},{96,112},{112,96},{1... | collective-permute-start | bytes 24584 | tf_op jit(solution)/shard_map/ppermute | solution.py:96
  204.6 7.3 %collective-permute-start.5 = (f32[2,1024]{1,0:T(2,128)S(1)}, f32[2,1024]{1,0:T(2,128)S(1)}, u32[]{:S(2)}, u32[]{:S(2)}) collective-permute-start(f32[2,1024]{1,0:T(2,128)S(1)} %pad_maximum_fusion.5), channel_id=1, source_target_pairs={{0,32},{16,48},{32,0},{48,16},{64,96},{80,112},{96,64},{112,80},{1... | collective-permute-start | bytes 24584 | tf_op jit(solution)/shard_map/ppermute | solution.py:96
  211.9 7.8 %collective-permute-start.6 = (f32[2,1024]{1,0:T(2,128)S(1)}, f32[2,1024]{1,0:T(2,128)S(1)}, u32[]{:S(2)}, u32[]{:S(2)}) collective-permute-start(f32[2,1024]{1,0:T(2,128)S(1)} %pad_maximum_fusion.6), channel_id=1, source_target_pairs={{0,64},{16,80},{32,96},{48,112},{64,0},{80,16},{96,32},{112,48},{1... | collective-permute-start | bytes 24584 | tf_op jit(solution)/shard_map/ppermute | solution.py:96
  219.8 6.4 %collective-permute-start.7 = (f32[2,1024]{1,0:T(2,128)S(1)}, f32[2,1024]{1,0:T(2,128)S(1)}, u32[]{:S(2)}, u32[]{:S(2)}) collective-permute-start(f32[2,1024]{1,0:T(2,128)S(1)} %pad_maximum_fusion.7), channel_id=1, source_target_pairs={{0,128},{16,144},{32,160},{48,176},{64,192},{80,208},{96,224},{112... | collective-permute-start | bytes 24584 | tf_op jit(solution)/shard_map/ppermute | solution.py:96
  226.3 11.4 %collective-permute-start.8 = (f32[2,1024]{1,0:T(2,128)S(1)}, f32[2,1024]{1,0:T(2,128)S(1)}, u32[]{:S(2)}, u32[]{:S(2)}) collective-permute-start(f32[2,1024]{1,0:T(2,128)S(1)} %pad_maximum_fusion.8), channel_id=1, source_target_pairs={{0,256},{16,272},{32,288},{48,304},{64,320},{80,336},{96,352},{112... | collective-permute-start | bytes 24584 | tf_op jit(solution)/shard_map/ppermute | solution.py:105
  233.9 9.5 %collective-permute-start.9 = (f32[2,1024]{1,0:T(2,128)S(1)}, f32[2,1024]{1,0:T(2,128)S(1)}, u32[]{:S(2)}, u32[]{:S(2)}) collective-permute-start(f32[2,1024]{1,0:T(2,128)S(1)} %pad_maximum_fusion.8), channel_id=1, source_target_pairs={{0,512},{16,528},{32,544},{48,560},{64,576},{80,592},{96,608},{112... | collective-permute-start | bytes 24584 | tf_op jit(solution)/shard_map/ppermute | solution.py:106
  243.7 0.8 copy-start.3
Sparse Core Ops, SparseCore 0:
  11.9 52.4 all-gather.1

commit v6 on v5

--- a/solution.py
+++ b/solution.py
@@ -65,7 +65,8 @@
 
 
 def pool(order, ids, counts, slots_t, hot_t, own_t):
-    blocks, bag_len, _ = slots_t.shape
+    blocks = order.shape[0]
+    bag_len = slots_t.shape[1]
     width = own_t.shape[0]
     grid_spec = pltpu.PrefetchScalarGridSpec(
         num_scalar_prefetch=3,
@@ -172,9 +173,12 @@
     own_t = table.T
     hot_t = jnp.take(own_t.reshape(row_width, -1, 128), panel_ids, axis=1).reshape(row_width, -1)
     gathered = lax.all_gather(hot_t, "cache", axis=0)
-    pooled = pool(source_block, ids, counts, slots_t, gathered, own_t)
-    pooled = pooled.reshape(feat_dev, caches, samp_dev, row_width)
-    features = lax.all_to_all(pooled, "cache", split_axis=1, concat_axis=0, tiled=True)[:, 0]
+    halves = []
+    for half in range(owner_blocks):
+        pooled = pool(source_block[half::owner_blocks], ids, counts, slots_t, gathered, own_t)
+        pooled = pooled.reshape(feat_dev, caches, 128, row_width)
+        halves.append(lax.all_to_all(pooled, "cache", split_axis=1, concat_axis=0, tiled=True)[:, 0])
+    features = jnp.concatenate(halves, axis=1)
     products = jnp.einsum("fne,gne->nfg", features, features, preferred_element_type=jnp.float32)
     interaction = (products / math.sqrt(row_width)).astype(jnp.bfloat16)
     flat_rows = interaction.reshape(interaction.shape[0], -1)

time: 253 us -> 243 us (0.960)
  blocking collectives: 72.1 us -> 0 us
  waiting for transfers between devices: 80.5 us -> 111 us
  starting transfers between devices: 40.8 us -> 61.1 us
  Pallas kernels: 31.8 us -> 39.5 us
  local copies, waits for them, and re-layouts: 6.98 us -> 11.9 us
    all_to_all x1 -> x0, blocking collectives: 72.1 us -> none  [shards(): lax.all_to_all(pooled, 'cache', split_axis=1, concat_axis=0, tiled=True)]
    all_to_all x0 -> x2, waiting for transfers between devices: none -> 30 us  [shards(): lax.all_to_all(pooled, 'cache', split_axis=1, concat_axis=0, tiled=True)]
    all_to_all x0 -> x2, starting transfers between devices: none -> 13 us  [shards(): lax.all_to_all(pooled, 'cache', split_axis=1, concat_axis=0, tiled=True)]
    ppermute x8, starting transfers between devices: 29.5 us -> 37.7 us  [merge_pair(): other = lax.ppermute(stats, axis, [(i, i ^ bit) for i in range(size)])]
    pallas_call x1 -> x2, Pallas kernels: 31.8 us -> 39.5 us  [pool(): pl.pallas_call(pool_kernel, grid_spec=grid_spec, out_shape=jax.ShapeDtype...]
    ppermute x1, waiting for transfers between devices: 0.01 us -> 7.44 us  [merge_three(): lax.ppermute(stats, axis, [(i, (i + stride) % size) for i in range(size)])]
    ppermute x1, waiting for transfers between devices: 5.74 us -> 0.01 us  [merge_three(): lax.ppermute(stats, axis, [(i, (i + 2 * stride) % size) for i in range(si...]
    ppermute x1, starting transfers between devices: 7.65 us -> 1.92 us  [merge_three(): lax.ppermute(stats, axis, [(i, (i + stride) % size) for i in range(size)])]
  transfers between devices with their start and end apart: 11 -> 13, of which waited for: 10 -> 12; matrix products, arithmetic and copies ran while one was open for 0% -> 1% of each run, Pallas kernels for 0% -> 8%
where the time goes in v6:
time: 243 us; the launch traced here: 242 us
  waiting for transfers between devices  111 us (46%)
  starting transfers between devices  61.1 us (25%)
  Pallas kernels  39.5 us (16%)
  between operations  14.5 us (6%)
  local copies, waits for them, and re-layouts  11.9 us (5%)
    all_gather x1, waiting for transfers between devices, shards(): gathered = lax.all_gather(hot_t, 'cache', axis=0)  51.2 us
    pallas_call x2, Pallas kernels, pool(): pl.pallas_call(pool_kernel, grid_spec=grid_spec, out_shape=jax.ShapeDtype...  39.5 us
    ppermute x8, starting transfers between devices, merge_pair(): other = lax.ppermute(stats, axis, [(i, i ^ bit) for i in range(size)])  37.7 us
    all_to_all x2, waiting for transfers between devices, shards(): lax.all_to_all(pooled, 'cache', split_axis=1, concat_axis=0, tiled=True)  30 us
    ppermute x8, waiting for transfers between devices, merge_pair(): other = lax.ppermute(stats, axis, [(i, i ^ bit) for i in range(size)])  22.6 us
    all_to_all x2, starting transfers between devices, shards(): lax.all_to_all(pooled, 'cache', split_axis=1, concat_axis=0, tiled=True)  13 us
    ppermute x1, starting transfers between devices, merge_three(): lax.ppermute(stats, axis, [(i, (i + 2 * stride) % size) for i in range(si...  8.5 us
    ppermute x1, waiting for transfers between devices, merge_three(): lax.ppermute(stats, axis, [(i, (i + stride) % size) for i in range(size)])  7.44 us
  transfers between devices with their start and end apart: 13, of which 12 were waited for; matrix products, arithmetic and copies ran while one was open for 1% of the time, Pallas kernels for 8%

profile of v6, /device:TPU:6, one launch (start us, length us, event | category | flops | bytes accessed | tf_op | source)
XLA Modules:
  0.0 242.4 jit_solution(3206335516282359886)
XLA Ops:
  8.7 1.3 copy.48
  11.0 0.8 copy.51
  13.2 51.2 %all-gather.2.cloned.1.call-done.hot_ref = bf16[16,256,384]{2,1,0:T(8,128)(2,1)} async-done(((bf16[1,256,384]{2,1,0:T(8,128)(2,1)}), bf16[16,256,384]{2,1,0:T(8,128)(2,1)}) %all-gather.2.cloned.1.call-update) | async-done | bytes 3145744 | tf_op jit(solution)/shard_map/all_gather | solution.py:175
  64.4 1.9 copy-done.1
  66.3 20.1 %shard_map.114 = bf16[2048,256]{1,0:T(8,128)(2,1)} custom-call(s32[16]{0:T(128)S(1)} %slice.84.order_ref, s32[512]{0:T(512)S(1)} %reshape.179.ids_ref, s32[32]{0:T(128)S(1)} %bitcast.48, s32[32,16,128]{2,1,0:T(8,128)S(1)} %bitcast.46, bf16[16,256,384]{2,1,0:T(8,128)(2,1)S(1)} %copy-done.1, bf16[256,1024]{1,0:T(8,128)(2,1)S(1)} %bitcast.44), custom_call_target="tpu_custom_call" | custom-call | tf_op jit(solution)/shard_map/pallas_call | solution.py:86
  86.4 5.7 %all-to-all-start.1 = ((bf16[1,16,128,256]{3,2,0,1:T(8,128)(2,1)}), bf16[1,16,128,256]{3,2,0,1:T(8,128)(2,1)S(1)}, u32[]{:S(2)}, u32[]{:S(2)}) async-start(bf16[1,16,128,256]{3,2,0,1:T(8,128)(2,1)} %bitcast.11), calls=%async_computation.1 | async-start | bytes 2097152 | tf_op jit(solution)/shard_map/all_to_all | solution.py:180
  92.2 1.9 copy-done.2
  94.1 19.4 %shard_map.113 = bf16[2048,256]{1,0:T(8,128)(2,1)} custom-call(s32[16]{0:T(128)S(1)} %slice.83.order_ref, s32[512]{0:T(512)S(1)} %reshape.179.ids_ref, s32[32]{0:T(128)S(1)} %bitcast.49, s32[32,16,128]{2,1,0:T(8,128)S(1)} %bitcast.47, bf16[16,256,384]{2,1,0:T(8,128)(2,1)S(1)} %copy-done.2, bf16[256,1024]{1,0:T(8,128)(2,1)S(1)} %bitcast.45), custom_call_target="tpu_custom_call" | custom-call | tf_op jit(solution)/shard_map/pallas_call | solution.py:86
  113.5 5.1 %all-to-all-done.1 = bf16[1,16,128,256]{3,2,0,1:T(8,128)(2,1)S(1)} async-done(((bf16[1,16,128,256]{3,2,0,1:T(8,128)(2,1)}), bf16[1,16,128,256]{3,2,0,1:T(8,128)(2,1)S(1)}, u32[]{:S(2)}, u32[]{:S(2)}) %all-to-all-start.1) | async-done | bytes 1048608 | tf_op jit(solution)/shard_map/all_to_all | solution.py:180
  118.6 7.2 %all-to-all-start = ((bf16[1,16,128,256]{3,2,0,1:T(8,128)(2,1)}), bf16[1,16,128,256]{3,2,0,1:T(8,128)(2,1)S(1)}, u32[]{:S(2)}, u32[]{:S(2)}) async-start(bf16[1,16,128,256]{3,2,0,1:T(8,128)(2,1)} %bitcast.8), calls=%async_computation | async-start | bytes 2097152 | tf_op jit(solution)/shard_map/all_to_all | solution.py:180
  125.9 1.6 copy.63
  127.4 24.9 %all-to-all-done = bf16[1,16,128,256]{3,2,0,1:T(8,128)(2,1)S(1)} async-done(((bf16[1,16,128,256]{3,2,0,1:T(8,128)(2,1)}), bf16[1,16,128,256]{3,2,0,1:T(8,128)(2,1)S(1)}, u32[]{:S(2)}, u32[]{:S(2)}) %all-to-all-start) | async-done | bytes 1048608 | tf_op jit(solution)/shard_map/all_to_all | solution.py:180
  154.3 1.0 copy.56
  155.8 3.8 %collective-permute-start = (f32[2,1024]{1,0:T(2,128)S(1)}, f32[2,1024]{1,0:T(2,128)S(1)}, u32[]{:S(2)}, u32[]{:S(2)}) collective-permute-start(f32[2,1024]{1,0:T(2,128)S(1)} %pad_maximum_fusion), channel_id=1, source_target_pairs={{0,1},{1,0},{2,3},{3,2},{4,5},{5,4},{6,7},{7,6},{8,9},{9,8},{10,11... | collective-permute-start | bytes 24584 | tf_op jit(solution)/shard_map/ppermute | solution.py:97
  160.5 1.9 collective-permute-start.1
  162.4 3.6 %collective-permute-done.1 = f32[2,1024]{1,0:T(2,128)S(1)} collective-permute-done((f32[2,1024]{1,0:T(2,128)S(1)}, f32[2,1024]{1,0:T(2,128)S(1)}, u32[]{:S(2)}, u32[]{:S(2)}) %collective-permute-start.1) | collective-permute-done | bytes 8224 | tf_op jit(solution)/shard_map/ppermute | solution.py:97
  166.1 2.3 collective-permute-start.2
  168.4 4.1 %collective-permute-done.2 = f32[2,1024]{1,0:T(2,128)S(1)} collective-permute-done((f32[2,1024]{1,0:T(2,128)S(1)}, f32[2,1024]{1,0:T(2,128)S(1)}, u32[]{:S(2)}, u32[]{:S(2)}) %collective-permute-start.2) | collective-permute-done | bytes 8224 | tf_op jit(solution)/shard_map/ppermute | solution.py:97
  172.6 3.9 %collective-permute-start.3 = (f32[2,1024]{1,0:T(2,128)S(1)}, f32[2,1024]{1,0:T(2,128)S(1)}, u32[]{:S(2)}, u32[]{:S(2)}) collective-permute-start(f32[2,1024]{1,0:T(2,128)S(1)} %pad_maximum_fusion.3), channel_id=1, source_target_pairs={{0,8},{1,9},{2,10},{3,11},{4,12},{5,13},{6,14},{7,15},{8,0},{9,1},... | collective-permute-start | bytes 24584 | tf_op jit(solution)/shard_map/ppermute | solution.py:97
  176.4 5.6 %collective-permute-done.3 = f32[2,1024]{1,0:T(2,128)S(1)} collective-permute-done((f32[2,1024]{1,0:T(2,128)S(1)}, f32[2,1024]{1,0:T(2,128)S(1)}, u32[]{:S(2)}, u32[]{:S(2)}) %collective-permute-start.3) | collective-permute-done | bytes 8224 | tf_op jit(solution)/shard_map/ppermute | solution.py:97
  182.0 4.3 %collective-permute-start.4 = (f32[2,1024]{1,0:T(2,128)S(1)}, f32[2,1024]{1,0:T(2,128)S(1)}, u32[]{:S(2)}, u32[]{:S(2)}) collective-permute-start(f32[2,1024]{1,0:T(2,128)S(1)} %pad_maximum_fusion.4), channel_id=1, source_target_pairs={{0,16},{16,0},{32,48},{48,32},{64,80},{80,64},{96,112},{112,96},{1... | collective-permute-start | bytes 24584 | tf_op jit(solution)/shard_map/ppermute | solution.py:97
  186.3 1.6 collective-permute-done.4
  188.0 11.8 %collective-permute-start.5 = (f32[2,1024]{1,0:T(2,128)S(1)}, f32[2,1024]{1,0:T(2,128)S(1)}, u32[]{:S(2)}, u32[]{:S(2)}) collective-permute-start(f32[2,1024]{1,0:T(2,128)S(1)} %pad_maximum_fusion.5), channel_id=1, source_target_pairs={{0,32},{16,48},{32,0},{48,16},{64,96},{80,112},{96,64},{112,80},{1... | collective-permute-start | bytes 24584 | tf_op jit(solution)/shard_map/ppermute | solution.py:97
  199.8 1.6 collective-permute-done.5
  201.4 1.9 collective-permute-start.6
  203.3 3.6 %collective-permute-done.6 = f32[2,1024]{1,0:T(2,128)S(1)} collective-permute-done((f32[2,1024]{1,0:T(2,128)S(1)}, f32[2,1024]{1,0:T(2,128)S(1)}, u32[]{:S(2)}, u32[]{:S(2)}) %collective-permute-start.6) | collective-permute-done | bytes 8224 | tf_op jit(solution)/shard_map/ppermute | solution.py:97
  207.0 7.8 %collective-permute-start.7 = (f32[2,1024]{1,0:T(2,128)S(1)}, f32[2,1024]{1,0:T(2,128)S(1)}, u32[]{:S(2)}, u32[]{:S(2)}) collective-permute-start(f32[2,1024]{1,0:T(2,128)S(1)} %pad_maximum_fusion.7), channel_id=1, source_target_pairs={{0,128},{16,144},{32,160},{48,176},{64,192},{80,208},{96,224},{112... | collective-permute-start | bytes 24584 | tf_op jit(solution)/shard_map/ppermute | solution.py:97
  214.8 1.6 collective-permute-done.7
  216.5 8.5 %collective-permute-start.9 = (f32[2,1024]{1,0:T(2,128)S(1)}, f32[2,1024]{1,0:T(2,128)S(1)}, u32[]{:S(2)}, u32[]{:S(2)}) collective-permute-start(f32[2,1024]{1,0:T(2,128)S(1)} %pad_maximum_fusion.8), channel_id=1, source_target_pairs={{0,512},{16,528},{32,544},{48,560},{64,576},{80,592},{96,608},{112... | collective-permute-start | bytes 24584 | tf_op jit(solution)/shard_map/ppermute | solution.py:107
  225.0 1.9 collective-permute-start.8
  227.0 7.4 %collective-permute-done.8 = f32[2,1024]{1,0:T(2,128)S(1)} collective-permute-done((f32[2,1024]{1,0:T(2,128)S(1)}, f32[2,1024]{1,0:T(2,128)S(1)}, u32[]{:S(2)}, u32[]{:S(2)}) %collective-permute-start.8) | collective-permute-done | bytes 8224 | tf_op jit(solution)/shard_map/ppermute | solution.py:106
  234.7 0.8 fusion.20
  (72 shorter events, 7.6 us)
Async XLA Ops:
  7.2 148.1 %copy-start = (bf16[256,1024]{1,0:T(8,128)(2,1)S(1)}, bf16[256,1024]{1,0:T(8,128)(2,1)}, u32[]{:S(2)}) copy-start(bf16[256,1024]{1,0:T(8,128)(2,1)} %param.16) | copy-start | bytes 1572868
  7.2 4.7 %copy-start.11 = (s32[16]{0:T(128)S(1)}, s32[16]{0:T(128)}, u32[]{:S(2)}) copy-start(s32[16]{0:T(128)} %param.15) | copy-start | bytes 196
  7.2 57.2 %all-gather.2.cloned.1.call-start = ((), (), s32[]{:S(2)}) async-start(), calls=%async_computation.2 | async-start | bytes 3342336 | tf_op jit(solution)/shard_map/all_gather | solution.py:175
  8.7 4.1 %copy-start.7 = (s32[1,32,16]{1,2,0:T(8,128)S(1)}, s32[1,32,16]{1,2,0:T(8,128)}, u32[]{:S(2)}) copy-start(s32[1,32,16]{1,2,0:T(8,128)} %param.13) | copy-start | bytes 6148
  8.7 4.3 %copy-start.6 = (s32[1,4096,16]{1,2,0:T(8,128)S(1)}, s32[1,4096,16]{1,2,0:T(8,128)}, u32[]{:S(2)}) copy-start(s32[1,4096,16]{1,2,0:T(8,128)} %param.12) | copy-start | bytes 786436
  10.0 54.4 %copy-start.3 = (s32[1,32]{1,0:T(1,128)S(1)}, s32[1,32]{1,0:T(1,128)}, u32[]{:S(2)}) copy-start(s32[1,32]{1,0:T(1,128)} %param.14) | copy-start | bytes 388
  64.4 1.9 copy-start.1
  86.4 32.2 %all-to-all-start.1 = ((bf16[1,16,128,256]{3,2,0,1:T(8,128)(2,1)}), bf16[1,16,128,256]{3,2,0,1:T(8,128)(2,1)S(1)}, u32[]{:S(2)}, u32[]{:S(2)}) async-start(bf16[1,16,128,256]{3,2,0,1:T(8,128)(2,1)} %bitcast.11), calls=%async_computation.1 | async-start | bytes 2097152 | tf_op jit(solution)/shard_map/all_to_all | solution.py:180
  92.2 1.9 copy-start.2
  118.6 33.7 %all-to-all-start = ((bf16[1,16,128,256]{3,2,0,1:T(8,128)(2,1)}), bf16[1,16,128,256]{3,2,0,1:T(8,128)(2,1)S(1)}, u32[]{:S(2)}, u32[]{:S(2)}) async-start(bf16[1,16,128,256]{3,2,0,1:T(8,128)(2,1)} %bitcast.8), calls=%async_computation | async-start | bytes 2097152 | tf_op jit(solution)/shard_map/all_to_all | solution.py:180
  152.3 1.2 copy-start.5
  155.3 71.7 %copy-start.10 = (bf16[1024]{0:T(1024)(128)(2,1)S(1)}, bf16[1024]{0:T(1024)(128)(2,1)}, u32[]{:S(2)}) copy-start(bf16[1024]{0:T(1024)(128)(2,1)} %param.19) | copy-start | bytes 6148
  155.3 79.2 %copy-start.8 = (f32[1024]{0:T(1024)S(1)}, f32[1024]{0:T(1024)}, u32[]{:S(2)}) copy-start(f32[1024]{0:T(1024)} %param.18) | copy-start | bytes 12292
  155.3 79.2 %copy-start.9 = (f32[1024]{0:T(1024)S(1)}, f32[1024]{0:T(1024)}, u32[]{:S(2)}) copy-start(f32[1024]{0:T(1024)} %param.17) | copy-start | bytes 12292
  155.8 4.6 %collective-permute-start = (f32[2,1024]{1,0:T(2,128)S(1)}, f32[2,1024]{1,0:T(2,128)S(1)}, u32[]{:S(2)}, u32[]{:S(2)}) collective-permute-start(f32[2,1024]{1,0:T(2,128)S(1)} %pad_maximum_fusion), channel_id=1, source_target_pairs={{0,1},{1,0},{2,3},{3,2},{4,5},{5,4},{6,7},{7,6},{8,9},{9,8},{10,11... | collective-permute-start | bytes 24584 | tf_op jit(solution)/shard_map/ppermute | solution.py:97
  160.5 5.5 %collective-permute-start.1 = (f32[2,1024]{1,0:T(2,128)S(1)}, f32[2,1024]{1,0:T(2,128)S(1)}, u32[]{:S(2)}, u32[]{:S(2)}) collective-permute-start(f32[2,1024]{1,0:T(2,128)S(1)} %pad_maximum_fusion.1), channel_id=1, source_target_pairs={{0,2},{1,3},{2,0},{3,1},{4,6},{5,7},{6,4},{7,5},{8,10},{9,11},{10,... | collective-permute-start | bytes 24584 | tf_op jit(solution)/shard_map/ppermute | solution.py:97
  166.1 6.4 %collective-permute-start.2 = (f32[2,1024]{1,0:T(2,128)S(1)}, f32[2,1024]{1,0:T(2,128)S(1)}, u32[]{:S(2)}, u32[]{:S(2)}) collective-permute-start(f32[2,1024]{1,0:T(2,128)S(1)} %pad_maximum_fusion.2), channel_id=1, source_target_pairs={{0,4},{1,5},{2,6},{3,7},{4,0},{5,1},{6,2},{7,3},{8,12},{9,13},{10,... | collective-permute-start | bytes 24584 | tf_op jit(solution)/shard_map/ppermute | solution.py:97
  172.6 9.5 %collective-permute-start.3 = (f32[2,1024]{1,0:T(2,128)S(1)}, f32[2,1024]{1,0:T(2,128)S(1)}, u32[]{:S(2)}, u32[]{:S(2)}) collective-permute-start(f32[2,1024]{1,0:T(2,128)S(1)} %pad_maximum_fusion.3), channel_id=1, source_target_pairs={{0,8},{1,9},{2,10},{3,11},{4,12},{5,13},{6,14},{7,15},{8,0},{9,1},... | collective-permute-start | bytes 24584 | tf_op jit(solution)/shard_map/ppermute | solution.py:97
  182.0 5.9 %collective-permute-start.4 = (f32[2,1024]{1,0:T(2,128)S(1)}, f32[2,1024]{1,0:T(2,128)S(1)}, u32[]{:S(2)}, u32[]{:S(2)}) collective-permute-start(f32[2,1024]{1,0:T(2,128)S(1)} %pad_maximum_fusion.4), channel_id=1, source_target_pairs={{0,16},{16,0},{32,48},{48,32},{64,80},{80,64},{96,112},{112,96},{1... | collective-permute-start | bytes 24584 | tf_op jit(solution)/shard_map/ppermute | solution.py:97
  188.0 13.4 %collective-permute-start.5 = (f32[2,1024]{1,0:T(2,128)S(1)}, f32[2,1024]{1,0:T(2,128)S(1)}, u32[]{:S(2)}, u32[]{:S(2)}) collective-permute-start(f32[2,1024]{1,0:T(2,128)S(1)} %pad_maximum_fusion.5), channel_id=1, source_target_pairs={{0,32},{16,48},{32,0},{48,16},{64,96},{80,112},{96,64},{112,80},{1... | collective-permute-start | bytes 24584 | tf_op jit(solution)/shard_map/ppermute | solution.py:97
  201.4 5.5 %collective-permute-start.6 = (f32[2,1024]{1,0:T(2,128)S(1)}, f32[2,1024]{1,0:T(2,128)S(1)}, u32[]{:S(2)}, u32[]{:S(2)}) collective-permute-start(f32[2,1024]{1,0:T(2,128)S(1)} %pad_maximum_fusion.6), channel_id=1, source_target_pairs={{0,64},{16,80},{32,96},{48,112},{64,0},{80,16},{96,32},{112,48},{1... | collective-permute-start | bytes 24584 | tf_op jit(solution)/shard_map/ppermute | solution.py:97
  207.0 9.4 %collective-permute-start.7 = (f32[2,1024]{1,0:T(2,128)S(1)}, f32[2,1024]{1,0:T(2,128)S(1)}, u32[]{:S(2)}, u32[]{:S(2)}) collective-permute-start(f32[2,1024]{1,0:T(2,128)S(1)} %pad_maximum_fusion.7), channel_id=1, source_target_pairs={{0,128},{16,144},{32,160},{48,176},{64,192},{80,208},{96,224},{112... | collective-permute-start | bytes 24584 | tf_op jit(solution)/shard_map/ppermute | solution.py:97
  216.5 10.5 %collective-permute-start.9 = (f32[2,1024]{1,0:T(2,128)S(1)}, f32[2,1024]{1,0:T(2,128)S(1)}, u32[]{:S(2)}, u32[]{:S(2)}) collective-permute-start(f32[2,1024]{1,0:T(2,128)S(1)} %pad_maximum_fusion.8), channel_id=1, source_target_pairs={{0,512},{16,528},{32,544},{48,560},{64,576},{80,592},{96,608},{112... | collective-permute-start | bytes 24584 | tf_op jit(solution)/shard_map/ppermute | solution.py:107
  225.0 9.5 %collective-permute-start.8 = (f32[2,1024]{1,0:T(2,128)S(1)}, f32[2,1024]{1,0:T(2,128)S(1)}, u32[]{:S(2)}, u32[]{:S(2)}) collective-permute-start(f32[2,1024]{1,0:T(2,128)S(1)} %pad_maximum_fusion.8), channel_id=1, source_target_pairs={{0,256},{16,272},{32,288},{48,304},{64,320},{80,336},{96,352},{112... | collective-permute-start | bytes 24584 | tf_op jit(solution)/shard_map/ppermute | solution.py:106
  234.7 0.8 copy-start.4
Sparse Core Ops, SparseCore 0:
  11.9 52.4 all-gather.1

commit v7 on v6

--- a/solution.py
+++ b/solution.py
@@ -177,12 +177,12 @@
     for half in range(owner_blocks):
         pooled = pool(source_block[half::owner_blocks], ids, counts, slots_t, gathered, own_t)
         pooled = pooled.reshape(feat_dev, caches, 128, row_width)
-        halves.append(lax.all_to_all(pooled, "cache", split_axis=1, concat_axis=0, tiled=True)[:, 0])
-    features = jnp.concatenate(halves, axis=1)
-    products = jnp.einsum("fne,gne->nfg", features, features, preferred_element_type=jnp.float32)
-    interaction = (products / math.sqrt(row_width)).astype(jnp.bfloat16)
-    flat_rows = interaction.reshape(interaction.shape[0], -1)
-    pre_norm = jnp.dot(flat_rows, top_weight, preferred_element_type=jnp.float32)
+        features = lax.all_to_all(pooled, "cache", split_axis=1, concat_axis=0, tiled=True)[:, 0]
+        products = jnp.einsum("fne,gne->nfg", features, features, preferred_element_type=jnp.float32)
+        interaction = (products / math.sqrt(row_width)).astype(jnp.bfloat16)
+        flat_rows = interaction.reshape(interaction.shape[0], -1)
+        halves.append(jnp.dot(flat_rows, top_weight, preferred_element_type=jnp.float32))
+    pre_norm = jnp.concatenate(halves, axis=0)
     col_mean, col_m2 = column_stats(pre_norm, (("cache", caches), ("shard", lax.axis_size("shard"))))
     col_var = col_m2 / (pre_norm.shape[0] * lax.axis_size("shard") * caches)
     normed = (pre_norm - col_mean) * lax.rsqrt(col_var + norm_eps) * bn_gain + bn_shift

time: 243 us -> 243 us (level)
  starting transfers between devices: 61.1 us -> 71 us
  Pallas kernels: 39.5 us -> 29.8 us
    pallas_call x2, Pallas kernels: 39.5 us -> 29.8 us  [pool(): pl.pallas_call(pool_kernel, grid_spec=grid_spec, out_shape=jax.ShapeDtype...]
    all_to_all x2, starting transfers between devices: 13 us -> 20.3 us  [shards(): lax.all_to_all(pooled, 'cache', split_axis=1, concat_axis=0, tiled=True)]
    ppermute x1, starting transfers between devices: 1.92 us -> 7.74 us  [merge_three(): lax.ppermute(stats, axis, [(i, (i + stride) % size) for i in range(size)])]
    ppermute x1, starting transfers between devices: 8.5 us -> 5.38 us  [merge_three(): lax.ppermute(stats, axis, [(i, (i + 2 * stride) % size) for i in range(si...]
    ppermute x1, waiting for transfers between devices: 7.44 us -> 4.49 us  [merge_three(): lax.ppermute(stats, axis, [(i, (i + stride) % size) for i in range(size)])]
    all_to_all x2, waiting for transfers between devices: 30 us -> 32.9 us  [shards(): lax.all_to_all(pooled, 'cache', split_axis=1, concat_axis=0, tiled=True)]
    unnamed x28 -> x26, local copies, waits for them, and re-layouts: 5.89 us -> 5.21 us
  transfers between devices with their start and end apart: 13 -> 13, of which waited for: 12 -> 12; matrix products, arithmetic and copies ran while one was open for 1% -> 2% of each run, Pallas kernels for 8% -> 6%
where the time goes in v7:
time: 243 us; the launch traced here: 241 us
  waiting for transfers between devices  110 us (45%)
  starting transfers between devices  71 us (29%)
  Pallas kernels  29.8 us (12%)
  between operations  14.5 us (6%)
  local copies, waits for them, and re-layouts  10.1 us (4%)
  matrix products  3.7 us (2%)
    all_gather x1, waiting for transfers between devices, shards(): gathered = lax.all_gather(hot_t, 'cache', axis=0)  51.2 us
    ppermute x8, starting transfers between devices, merge_pair(): other = lax.ppermute(stats, axis, [(i, i ^ bit) for i in range(size)])  37.6 us
    all_to_all x2, waiting for transfers between devices, shards(): lax.all_to_all(pooled, 'cache', split_axis=1, concat_axis=0, tiled=True)  32.9 us
    pallas_call x2, Pallas kernels, pool(): pl.pallas_call(pool_kernel, grid_spec=grid_spec, out_shape=jax.ShapeDtype...  29.8 us
    ppermute x8, waiting for transfers between devices, merge_pair(): other = lax.ppermute(stats, axis, [(i, i ^ bit) for i in range(size)])  21.3 us
    all_to_all x2, starting transfers between devices, shards(): lax.all_to_all(pooled, 'cache', split_axis=1, concat_axis=0, tiled=True)  20.3 us
    ppermute x1, starting transfers between devices, merge_three(): lax.ppermute(stats, axis, [(i, (i + stride) % size) for i in range(size)])  7.74 us
    ppermute x1, starting transfers between devices, merge_three(): lax.ppermute(stats, axis, [(i, (i + 2 * stride) % size) for i in range(si...  5.38 us
  transfers between devices with their start and end apart: 13, of which 12 were waited for; matrix products, arithmetic and copies ran while one was open for 2% of the time, Pallas kernels for 6%

profile of v7, /device:TPU:6, one launch (start us, length us, event | category | flops | bytes accessed | tf_op | source)
XLA Modules:
  0.0 241.5 jit_solution(16190463286449142293)
XLA Ops:
  8.7 1.2 copy.51
  11.0 0.8 copy.54
  13.2 51.2 %all-gather.2.cloned.1.call-done.hot_ref = bf16[16,256,384]{2,1,0:T(8,128)(2,1)} async-done(((bf16[1,256,384]{2,1,0:T(8,128)(2,1)}), bf16[16,256,384]{2,1,0:T(8,128)(2,1)}) %all-gather.2.cloned.1.call-update) | async-done | bytes 3145744 | tf_op jit(solution)/shard_map/all_gather | solution.py:175
  64.4 1.9 copy-done.1
  66.3 15.1 %shard_map.114 = bf16[2048,256]{1,0:T(8,128)(2,1)} custom-call(s32[16]{0:T(128)S(1)} %slice.84.order_ref, s32[512]{0:T(512)S(1)} %reshape.206.ids_ref, s32[32]{0:T(128)S(1)} %bitcast.51, s32[32,16,128]{2,1,0:T(8,128)S(1)} %bitcast.49, bf16[16,256,384]{2,1,0:T(8,128)(2,1)S(1)} %copy-done.1, bf16[256,1024]{1,0:T(8,128)(2,1)S(1)} %bitcast.47), custom_call_target="tpu_custom_call" | custom-call | tf_op jit(solution)/shard_map/pallas_call | solution.py:86
  81.4 13.2 %all-to-all-start.1 = ((bf16[1,16,128,256]{3,2,0,1:T(8,128)(2,1)}), bf16[1,16,128,256]{3,2,0,1:T(8,128)(2,1)S(1)}, u32[]{:S(2)}, u32[]{:S(2)}) async-start(bf16[1,16,128,256]{3,2,0,1:T(8,128)(2,1)} %bitcast.12), calls=%async_computation.1 | async-start | bytes 2097152 | tf_op jit(solution)/shard_map/all_to_all | solution.py:180
  94.7 1.9 copy-done.2
  96.6 14.7 %shard_map.113 = bf16[2048,256]{1,0:T(8,128)(2,1)} custom-call(s32[16]{0:T(128)S(1)} %slice.83.order_ref, s32[512]{0:T(512)S(1)} %reshape.206.ids_ref, s32[32]{0:T(128)S(1)} %bitcast.52, s32[32,16,128]{2,1,0:T(8,128)S(1)} %bitcast.50, bf16[16,256,384]{2,1,0:T(8,128)(2,1)S(1)} %copy-done.2, bf16[256,1024]{1,0:T(8,128)(2,1)S(1)} %bitcast.48), custom_call_target="tpu_custom_call" | custom-call | tf_op jit(solution)/shard_map/pallas_call | solution.py:86
  111.3 9.8 %all-to-all-done.1 = bf16[1,16,128,256]{3,2,0,1:T(8,128)(2,1)S(1)} async-done(((bf16[1,16,128,256]{3,2,0,1:T(8,128)(2,1)}), bf16[1,16,128,256]{3,2,0,1:T(8,128)(2,1)S(1)}, u32[]{:S(2)}, u32[]{:S(2)}) %all-to-all-start.1) | async-done | bytes 1048608 | tf_op jit(solution)/shard_map/all_to_all | solution.py:180
  121.1 7.1 %all-to-all-start = ((bf16[1,16,128,256]{3,2,0,1:T(8,128)(2,1)}), bf16[1,16,128,256]{3,2,0,1:T(8,128)(2,1)S(1)}, u32[]{:S(2)}, u32[]{:S(2)}) async-start(bf16[1,16,128,256]{3,2,0,1:T(8,128)(2,1)} %bitcast.8), calls=%async_computation | async-start | bytes 2097152 | tf_op jit(solution)/shard_map/all_to_all | solution.py:180
  128.2 1.7 fusion
  129.9 1.6 copy.60
  131.5 23.2 %all-to-all-done = bf16[1,16,128,256]{3,2,0,1:T(8,128)(2,1)S(1)} async-done(((bf16[1,16,128,256]{3,2,0,1:T(8,128)(2,1)}), bf16[1,16,128,256]{3,2,0,1:T(8,128)(2,1)S(1)}, u32[]{:S(2)}, u32[]{:S(2)}) %all-to-all-start) | async-done | bytes 1048608 | tf_op jit(solution)/shard_map/all_to_all | solution.py:180
  156.5 3.8 %collective-permute-start = (f32[2,1024]{1,0:T(2,128)S(1)}, f32[2,1024]{1,0:T(2,128)S(1)}, u32[]{:S(2)}, u32[]{:S(2)}) collective-permute-start(f32[2,1024]{1,0:T(2,128)S(1)} %pad_maximum_fusion.1), channel_id=1, source_target_pairs={{0,1},{1,0},{2,3},{3,2},{4,5},{5,4},{6,7},{7,6},{8,9},{9,8},{10,11... | collective-permute-start | bytes 24584 | tf_op jit(solution)/shard_map/ppermute | solution.py:97
  161.2 1.9 collective-permute-start.1
  163.1 3.6 %collective-permute-done.1 = f32[2,1024]{1,0:T(2,128)S(1)} collective-permute-done((f32[2,1024]{1,0:T(2,128)S(1)}, f32[2,1024]{1,0:T(2,128)S(1)}, u32[]{:S(2)}, u32[]{:S(2)}) %collective-permute-start.1) | collective-permute-done | bytes 8224 | tf_op jit(solution)/shard_map/ppermute | solution.py:97
  166.8 2.3 collective-permute-start.2
  169.1 4.1 %collective-permute-done.2 = f32[2,1024]{1,0:T(2,128)S(1)} collective-permute-done((f32[2,1024]{1,0:T(2,128)S(1)}, f32[2,1024]{1,0:T(2,128)S(1)}, u32[]{:S(2)}, u32[]{:S(2)}) %collective-permute-start.2) | collective-permute-done | bytes 8224 | tf_op jit(solution)/shard_map/ppermute | solution.py:97
  173.3 3.9 %collective-permute-start.3 = (f32[2,1024]{1,0:T(2,128)S(1)}, f32[2,1024]{1,0:T(2,128)S(1)}, u32[]{:S(2)}, u32[]{:S(2)}) collective-permute-start(f32[2,1024]{1,0:T(2,128)S(1)} %pad_maximum_fusion.4), channel_id=1, source_target_pairs={{0,8},{1,9},{2,10},{3,11},{4,12},{5,13},{6,14},{7,15},{8,0},{9,1},... | collective-permute-start | bytes 24584 | tf_op jit(solution)/shard_map/ppermute | solution.py:97
  177.2 5.6 %collective-permute-done.3 = f32[2,1024]{1,0:T(2,128)S(1)} collective-permute-done((f32[2,1024]{1,0:T(2,128)S(1)}, f32[2,1024]{1,0:T(2,128)S(1)}, u32[]{:S(2)}, u32[]{:S(2)}) %collective-permute-start.3) | collective-permute-done | bytes 8224 | tf_op jit(solution)/shard_map/ppermute | solution.py:97
  182.8 3.7 %collective-permute-start.4 = (f32[2,1024]{1,0:T(2,128)S(1)}, f32[2,1024]{1,0:T(2,128)S(1)}, u32[]{:S(2)}, u32[]{:S(2)}) collective-permute-start(f32[2,1024]{1,0:T(2,128)S(1)} %pad_maximum_fusion.5), channel_id=1, source_target_pairs={{0,16},{16,0},{32,48},{48,32},{64,80},{80,64},{96,112},{112,96},{1... | collective-permute-start | bytes 24584 | tf_op jit(solution)/shard_map/ppermute | solution.py:97
  186.5 1.8 collective-permute-done.4
  188.3 4.9 %collective-permute-start.5 = (f32[2,1024]{1,0:T(2,128)S(1)}, f32[2,1024]{1,0:T(2,128)S(1)}, u32[]{:S(2)}, u32[]{:S(2)}) collective-permute-start(f32[2,1024]{1,0:T(2,128)S(1)} %pad_maximum_fusion.6), channel_id=1, source_target_pairs={{0,32},{16,48},{32,0},{48,16},{64,96},{80,112},{96,64},{112,80},{1... | collective-permute-start | bytes 24584 | tf_op jit(solution)/shard_map/ppermute | solution.py:97
  193.2 2.2 collective-permute-done.5
  195.4 10.7 %collective-permute-start.6 = (f32[2,1024]{1,0:T(2,128)S(1)}, f32[2,1024]{1,0:T(2,128)S(1)}, u32[]{:S(2)}, u32[]{:S(2)}) collective-permute-start(f32[2,1024]{1,0:T(2,128)S(1)} %pad_maximum_fusion.7), channel_id=1, source_target_pairs={{0,64},{16,80},{32,96},{48,112},{64,0},{80,16},{96,32},{112,48},{1... | collective-permute-start | bytes 24584 | tf_op jit(solution)/shard_map/ppermute | solution.py:97
  206.1 1.6 collective-permute-done.6
  207.8 6.3 %collective-permute-start.7 = (f32[2,1024]{1,0:T(2,128)S(1)}, f32[2,1024]{1,0:T(2,128)S(1)}, u32[]{:S(2)}, u32[]{:S(2)}) collective-permute-start(f32[2,1024]{1,0:T(2,128)S(1)} %pad_maximum_fusion.8), channel_id=1, source_target_pairs={{0,128},{16,144},{32,160},{48,176},{64,192},{80,208},{96,224},{112... | collective-permute-start | bytes 24584 | tf_op jit(solution)/shard_map/ppermute | solution.py:97
  214.1 1.6 collective-permute-done.7
  215.8 5.4 %collective-permute-start.9 = (f32[2,1024]{1,0:T(2,128)S(1)}, f32[2,1024]{1,0:T(2,128)S(1)}, u32[]{:S(2)}, u32[]{:S(2)}) collective-permute-start(f32[2,1024]{1,0:T(2,128)S(1)} %pad_maximum_fusion.9), channel_id=1, source_target_pairs={{0,512},{16,528},{32,544},{48,560},{64,576},{80,592},{96,608},{112... | collective-permute-start | bytes 24584 | tf_op jit(solution)/shard_map/ppermute | solution.py:107
  221.2 7.7 %collective-permute-start.8 = (f32[2,1024]{1,0:T(2,128)S(1)}, f32[2,1024]{1,0:T(2,128)S(1)}, u32[]{:S(2)}, u32[]{:S(2)}) collective-permute-start(f32[2,1024]{1,0:T(2,128)S(1)} %pad_maximum_fusion.9), channel_id=1, source_target_pairs={{0,256},{16,272},{32,288},{48,304},{64,320},{80,336},{96,352},{112... | collective-permute-start | bytes 24584 | tf_op jit(solution)/shard_map/ppermute | solution.py:106
  229.0 4.5 %collective-permute-done.8 = f32[2,1024]{1,0:T(2,128)S(1)} collective-permute-done((f32[2,1024]{1,0:T(2,128)S(1)}, f32[2,1024]{1,0:T(2,128)S(1)}, u32[]{:S(2)}, u32[]{:S(2)}) %collective-permute-start.8) | collective-permute-done | bytes 8224 | tf_op jit(solution)/shard_map/ppermute | solution.py:106
  233.8 0.8 fusion.22
  (72 shorter events, 7.1 us)
Async XLA Ops:
  7.2 148.7 %copy-start = (bf16[256,1024]{1,0:T(8,128)(2,1)S(1)}, bf16[256,1024]{1,0:T(8,128)(2,1)}, u32[]{:S(2)}) copy-start(bf16[256,1024]{1,0:T(8,128)(2,1)} %param.16) | copy-start | bytes 1572868
  7.2 4.7 %copy-start.10 = (s32[16]{0:T(128)S(1)}, s32[16]{0:T(128)}, u32[]{:S(2)}) copy-start(s32[16]{0:T(128)} %param.15) | copy-start | bytes 196
  7.2 5.6 %copy-start.6 = (s32[1,32,16]{1,2,0:T(8,128)S(1)}, s32[1,32,16]{1,2,0:T(8,128)}, u32[]{:S(2)}) copy-start(s32[1,32,16]{1,2,0:T(8,128)} %param.13) | copy-start | bytes 6148
  7.2 5.7 %copy-start.5 = (s32[1,4096,16]{1,2,0:T(8,128)S(1)}, s32[1,4096,16]{1,2,0:T(8,128)}, u32[]{:S(2)}) copy-start(s32[1,4096,16]{1,2,0:T(8,128)} %param.12) | copy-start | bytes 786436
  7.2 57.2 %copy-start.3 = (s32[1,32]{1,0:T(1,128)S(1)}, s32[1,32]{1,0:T(1,128)}, u32[]{:S(2)}) copy-start(s32[1,32]{1,0:T(1,128)} %param.14) | copy-start | bytes 388
  7.2 57.2 %all-gather.2.cloned.1.call-start = ((), (), s32[]{:S(2)}) async-start(), calls=%async_computation.2 | async-start | bytes 3342336 | tf_op jit(solution)/shard_map/all_gather | solution.py:175
  64.4 1.9 copy-start.1
  81.4 39.7 %all-to-all-start.1 = ((bf16[1,16,128,256]{3,2,0,1:T(8,128)(2,1)}), bf16[1,16,128,256]{3,2,0,1:T(8,128)(2,1)S(1)}, u32[]{:S(2)}, u32[]{:S(2)}) async-start(bf16[1,16,128,256]{3,2,0,1:T(8,128)(2,1)} %bitcast.12), calls=%async_computation.1 | async-start | bytes 2097152 | tf_op jit(solution)/shard_map/all_to_all | solution.py:180
  94.7 1.9 copy-start.2
  121.1 33.6 %all-to-all-start = ((bf16[1,16,128,256]{3,2,0,1:T(8,128)(2,1)}), bf16[1,16,128,256]{3,2,0,1:T(8,128)(2,1)S(1)}, u32[]{:S(2)}, u32[]{:S(2)}) async-start(bf16[1,16,128,256]{3,2,0,1:T(8,128)(2,1)} %bitcast.8), calls=%async_computation | async-start | bytes 2097152 | tf_op jit(solution)/shard_map/all_to_all | solution.py:180
  131.5 97.5 %copy-start.9 = (bf16[1024]{0:T(1024)(128)(2,1)S(1)}, bf16[1024]{0:T(1024)(128)(2,1)}, u32[]{:S(2)}) copy-start(bf16[1024]{0:T(1024)(128)(2,1)} %param.19) | copy-start | bytes 6148
  131.5 102.1 %copy-start.7 = (f32[1024]{0:T(1024)S(1)}, f32[1024]{0:T(1024)}, u32[]{:S(2)}) copy-start(f32[1024]{0:T(1024)} %param.18) | copy-start | bytes 12292
  131.5 102.1 %copy-start.8 = (f32[1024]{0:T(1024)S(1)}, f32[1024]{0:T(1024)}, u32[]{:S(2)}) copy-start(f32[1024]{0:T(1024)} %param.17) | copy-start | bytes 12292
  156.5 4.6 %collective-permute-start = (f32[2,1024]{1,0:T(2,128)S(1)}, f32[2,1024]{1,0:T(2,128)S(1)}, u32[]{:S(2)}, u32[]{:S(2)}) collective-permute-start(f32[2,1024]{1,0:T(2,128)S(1)} %pad_maximum_fusion.1), channel_id=1, source_target_pairs={{0,1},{1,0},{2,3},{3,2},{4,5},{5,4},{6,7},{7,6},{8,9},{9,8},{10,11... | collective-permute-start | bytes 24584 | tf_op jit(solution)/shard_map/ppermute | solution.py:97
  161.2 5.5 %collective-permute-start.1 = (f32[2,1024]{1,0:T(2,128)S(1)}, f32[2,1024]{1,0:T(2,128)S(1)}, u32[]{:S(2)}, u32[]{:S(2)}) collective-permute-start(f32[2,1024]{1,0:T(2,128)S(1)} %pad_maximum_fusion.2), channel_id=1, source_target_pairs={{0,2},{1,3},{2,0},{3,1},{4,6},{5,7},{6,4},{7,5},{8,10},{9,11},{10,... | collective-permute-start | bytes 24584 | tf_op jit(solution)/shard_map/ppermute | solution.py:97
  166.8 6.4 %collective-permute-start.2 = (f32[2,1024]{1,0:T(2,128)S(1)}, f32[2,1024]{1,0:T(2,128)S(1)}, u32[]{:S(2)}, u32[]{:S(2)}) collective-permute-start(f32[2,1024]{1,0:T(2,128)S(1)} %pad_maximum_fusion.3), channel_id=1, source_target_pairs={{0,4},{1,5},{2,6},{3,7},{4,0},{5,1},{6,2},{7,3},{8,12},{9,13},{10,... | collective-permute-start | bytes 24584 | tf_op jit(solution)/shard_map/ppermute | solution.py:97
  173.3 9.5 %collective-permute-start.3 = (f32[2,1024]{1,0:T(2,128)S(1)}, f32[2,1024]{1,0:T(2,128)S(1)}, u32[]{:S(2)}, u32[]{:S(2)}) collective-permute-start(f32[2,1024]{1,0:T(2,128)S(1)} %pad_maximum_fusion.4), channel_id=1, source_target_pairs={{0,8},{1,9},{2,10},{3,11},{4,12},{5,13},{6,14},{7,15},{8,0},{9,1},... | collective-permute-start | bytes 24584 | tf_op jit(solution)/shard_map/ppermute | solution.py:97
  182.8 5.5 %collective-permute-start.4 = (f32[2,1024]{1,0:T(2,128)S(1)}, f32[2,1024]{1,0:T(2,128)S(1)}, u32[]{:S(2)}, u32[]{:S(2)}) collective-permute-start(f32[2,1024]{1,0:T(2,128)S(1)} %pad_maximum_fusion.5), channel_id=1, source_target_pairs={{0,16},{16,0},{32,48},{48,32},{64,80},{80,64},{96,112},{112,96},{1... | collective-permute-start | bytes 24584 | tf_op jit(solution)/shard_map/ppermute | solution.py:97
  188.3 7.0 %collective-permute-start.5 = (f32[2,1024]{1,0:T(2,128)S(1)}, f32[2,1024]{1,0:T(2,128)S(1)}, u32[]{:S(2)}, u32[]{:S(2)}) collective-permute-start(f32[2,1024]{1,0:T(2,128)S(1)} %pad_maximum_fusion.6), channel_id=1, source_target_pairs={{0,32},{16,48},{32,0},{48,16},{64,96},{80,112},{96,64},{112,80},{1... | collective-permute-start | bytes 24584 | tf_op jit(solution)/shard_map/ppermute | solution.py:97
  195.4 12.3 %collective-permute-start.6 = (f32[2,1024]{1,0:T(2,128)S(1)}, f32[2,1024]{1,0:T(2,128)S(1)}, u32[]{:S(2)}, u32[]{:S(2)}) collective-permute-start(f32[2,1024]{1,0:T(2,128)S(1)} %pad_maximum_fusion.7), channel_id=1, source_target_pairs={{0,64},{16,80},{32,96},{48,112},{64,0},{80,16},{96,32},{112,48},{1... | collective-permute-start | bytes 24584 | tf_op jit(solution)/shard_map/ppermute | solution.py:97
  207.8 8.0 %collective-permute-start.7 = (f32[2,1024]{1,0:T(2,128)S(1)}, f32[2,1024]{1,0:T(2,128)S(1)}, u32[]{:S(2)}, u32[]{:S(2)}) collective-permute-start(f32[2,1024]{1,0:T(2,128)S(1)} %pad_maximum_fusion.8), channel_id=1, source_target_pairs={{0,128},{16,144},{32,160},{48,176},{64,192},{80,208},{96,224},{112... | collective-permute-start | bytes 24584 | tf_op jit(solution)/shard_map/ppermute | solution.py:97
  215.8 13.2 %collective-permute-start.9 = (f32[2,1024]{1,0:T(2,128)S(1)}, f32[2,1024]{1,0:T(2,128)S(1)}, u32[]{:S(2)}, u32[]{:S(2)}) collective-permute-start(f32[2,1024]{1,0:T(2,128)S(1)} %pad_maximum_fusion.9), channel_id=1, source_target_pairs={{0,512},{16,528},{32,544},{48,560},{64,576},{80,592},{96,608},{112... | collective-permute-start | bytes 24584 | tf_op jit(solution)/shard_map/ppermute | solution.py:107
  221.2 12.3 %collective-permute-start.8 = (f32[2,1024]{1,0:T(2,128)S(1)}, f32[2,1024]{1,0:T(2,128)S(1)}, u32[]{:S(2)}, u32[]{:S(2)}) collective-permute-start(f32[2,1024]{1,0:T(2,128)S(1)} %pad_maximum_fusion.9), channel_id=1, source_target_pairs={{0,256},{16,272},{32,288},{48,304},{64,320},{80,336},{96,352},{112... | collective-permute-start | bytes 24584 | tf_op jit(solution)/shard_map/ppermute | solution.py:106
  233.8 0.8 copy-start.4
Sparse Core Ops, SparseCore 0:
  11.9 52.4 all-gather.1
